TPU v7x, 128 devices: a whole 4x4x4 slice. The times are simulated.
128 devices in a mesh: seq: 32 (over y, z, core), head: 4 (over x).
Axes of the slice: x: 4, y: 4, z: 4, core: 2. Of those that a mesh axis runs over, the one named last changes fastest.
Arguments:
- queries: bfloat16 [16384, 2048], P('seq', 'head'), may hold values from -6 to 6
- key_pairs: bfloat16 [16384, 2, 2048], P('seq', None, 'head'), may hold values from -6 to 6
- value_pairs: bfloat16 [16384, 2, 2048], P('seq', None, 'head'), may hold values from -0.1875 to 0.1875
- init_state: float32 [16, 128, 128], P('head'), may hold values from -6 to 6
- out_weight: bfloat16 [2048, 2048], replicated, may hold values from -0.125 to 0.125
Outputs:
- projected: bfloat16 [16384, 2048], P('seq', 'head')
All inputs are finite; a program needn't handle non-finite values.
Results may differ from a plain program's by a relative error of at most 0.0085.
Values may be sent and summed in bfloat16 or wider, within the bound.
No kernel may reach another device: no remote copies, remote signals or barrier semaphores. Data moves between devices by JAX's collectives and lax.ppermute only.
A program may use at most 128 MiB of HBM per device.

v0:
```python
import jax
import jax.numpy as jnp
from jax import lax
from jax.sharding import PartitionSpec as P

HEAD_DIM = 128
BLOCK = 32


epsilon = 1e-06


def carried_in(part, axis, combine, identity):
    place = lax.axis_index(axis)
    gathered = jax.tree.map(lambda a: lax.all_gather(a, axis), part)
    state = jax.tree.map(lambda a, e: jnp.zeros_like(a) + jnp.asarray(e, a.dtype), part, identity)

    def one(hop, state):
        return combine(
            state, jax.tree.map(lambda a: lax.dynamic_index_in_dim(a, hop, 0, False), gathered)
        )

    return lax.fori_loop(0, place, one, state)


def product(left, right, pattern):
    return jnp.einsum(pattern, left, right, precision=lax.Precision.HIGHEST)


def unit_rows(entries):
    return entries * lax.rsqrt(jnp.sum(entries * entries, axis=-1, keepdims=True) + epsilon)


def block_parts(query_block, key_block, value_block):
    query_block = unit_rows(query_block.astype(jnp.float32))
    key_block = unit_rows(key_block.astype(jnp.float32))
    value_block = value_block.astype(jnp.float32)
    state_width = key_block.shape[-1]
    micro_len = key_block.shape[-2]
    gram = product(key_block, key_block, "...id,...jd->...ij")
    strict = jnp.tril(jnp.ones((micro_len, micro_len), jnp.float32), -1)
    system = jnp.eye(micro_len, dtype=jnp.float32) + 2.0 * gram * strict
    stacked = 2.0 * jnp.concatenate([key_block, value_block], axis=-1)
    solved = jax.scipy.linalg.solve_triangular(system, stacked, lower=True, unit_diagonal=True)
    writes = solved[..., :state_width]
    updates = solved[..., state_width:]
    scores = product(query_block, key_block, "...id,...jd->...ij")
    row_index = lax.broadcasted_iota(jnp.int32, (query_block.shape[-2], micro_len), 0)
    col_index = lax.broadcasted_iota(jnp.int32, (query_block.shape[-2], micro_len), 1)
    scores = jnp.where(col_index <= 2 * row_index + 1, scores, jnp.zeros_like(scores))
    adjusted = query_block - product(scores, writes, "...ij,...jd->...id")
    inside = product(scores, updates, "...ij,...jd->...id")
    moving = jnp.eye(state_width, dtype=jnp.float32) - product(
        key_block, writes, "...cd,...ce->...de"
    )
    carried = product(key_block, updates, "...cd,...ce->...de")
    return (adjusted, inside, moving, carried)


def compose(earlier, later):
    return (
        product(later[0], earlier[0], "...ij,...jk->...ik"),
        product(later[0], earlier[1], "...ij,...jk->...ik") + later[1],
    )


def advance_map(running_map, pieces):
    return (compose(running_map, pieces), running_map)


def local(queries, key_pairs, value_pairs, init_state, out_weight):
    tokens = queries.shape[0]
    head_count = queries.shape[1] // HEAD_DIM
    blocks = tokens // BLOCK
    state_width = HEAD_DIM
    query_blocks = jnp.transpose(queries.reshape(blocks, BLOCK, head_count, HEAD_DIM), (2, 0, 1, 3))
    key_blocks = jnp.transpose(
        key_pairs.reshape(blocks, 2 * BLOCK, head_count, HEAD_DIM), (2, 0, 1, 3)
    )
    value_blocks = jnp.transpose(
        value_pairs.reshape(blocks, 2 * BLOCK, head_count, HEAD_DIM), (2, 0, 1, 3)
    )
    adjusted, inside, moving, carried = block_parts(query_blocks, key_blocks, value_blocks)
    per_group = 8
    group_count = blocks // per_group

    def grouped(array):
        shaped = array.reshape((head_count, group_count, per_group) + array.shape[2:])
        return jnp.moveaxis(shaped, 2, 0)

    identity = jnp.eye(state_width, dtype=jnp.float32)
    group_identity = jnp.broadcast_to(identity, (head_count, group_count, state_width, state_width))
    group_zeros = jnp.zeros((head_count, group_count, state_width, state_width), jnp.float32)
    group_map, start_map = lax.scan(
        advance_map, (group_identity, group_zeros), (grouped(moving), grouped(carried))
    )
    start_move = jnp.moveaxis(start_map[0], 0, 2)
    start_carry = jnp.moveaxis(start_map[1], 0, 2)
    head_identity = jnp.broadcast_to(identity, (head_count, state_width, state_width))
    head_zeros = jnp.zeros((head_count, state_width, state_width), jnp.float32)
    shard_map_pair, prior_map = lax.scan(
        advance_map,
        (head_identity, head_zeros),
        (jnp.moveaxis(group_map[0], 1, 0), jnp.moveaxis(group_map[1], 1, 0)),
    )
    prior_move = jnp.moveaxis(prior_map[0], 0, 1)
    prior_carry = jnp.moveaxis(prior_map[1], 0, 1)
    query_grouped = adjusted.reshape(head_count, group_count, per_group, BLOCK, state_width)
    inside_grouped = inside.reshape(head_count, group_count, per_group, BLOCK, state_width)
    before_move, before_carry = carried_in(
        (shard_map_pair[0], shard_map_pair[1]), "seq", compose, (head_identity, head_zeros)
    )
    entering = product(before_move, init_state, "hij,hjk->hik") + before_carry
    group_state = product(prior_move, entering, "hgij,hjk->hgik") + prior_carry
    block_state = product(start_move, group_state, "hgpij,hgjk->hgpik") + start_carry
    attended_grouped = product(query_grouped, block_state, "hgpcd,hgpde->hgpce") + inside_grouped
    attended_heads = attended_grouped.reshape(head_count, blocks, BLOCK, state_width)
    attended = (
        jnp.transpose(attended_heads, (1, 2, 0, 3))
        .reshape(tokens, head_count * state_width)
        .astype(jnp.bfloat16)
    )
    model_cols = out_weight.shape[1] // lax.axis_size("head")
    own_cols = lax.dynamic_slice_in_dim(
        out_weight, lax.axis_index("head") * model_cols, model_cols, 1
    )
    return jnp.dot(
        lax.all_gather(attended, "head", axis=1, tiled=True),
        own_cols,
        preferred_element_type=jnp.float32,
    ).astype(jnp.bfloat16)


def solution(mesh):
    in_specs = (
        P("seq", "head"),
        P("seq", None, "head"),
        P("seq", None, "head"),
        P("head", None, None),
        P(),
    )
    out_specs = P("seq", "head")
    return jax.shard_map(local, mesh=mesh, in_specs=in_specs, out_specs=out_specs, check_vma=False)
```

profile of v0, /device:TPU:16, one launch (start us, length us, event | category | flops | bytes accessed | tf_op | source)
XLA Modules:
  0.0 679.1 jit_solution(15191085395185680069)
XLA Ops:
  7.3 2.1 reshape.80
  10.8 2.1 bitcast_multiply_fusion
  14.9 3.2 copy.61
  18.1 4.7 add_bitcast_fusion
  22.8 316.5 %custom-call.4 = f32[4,16,1,64,64]{3,4,2,1,0:T(8,128)} custom-call(f32[4,16,1,64,64]{4,3,2,1,0:T(8,128)} %add_bitcast_fusion), custom_call_target="InvertDiagBlocksLowerTriangular" | custom-call | tf_op jit(solution)/shard_map/jit(_solve_triangular)/vmap(vmap())/triangular_solve | solution.py:44
  339.3 6.1 fusion.29
  345.5 6.7 fusion.45
  352.2 6.9 %convolution_subtract_fusion = f32[4,16,128,128]{3,2,1,0:T(8,128)S(1)} fusion(f32[4,16,64,128]{3,2,1,0:T(8,128)S(1)} %bitcast_multiply_fusion, f32[128,128]{1,0:T(8,128)S(1)} %fusion.69, f32[4,16,64,256]{3,2,1,0:T(8,128)S(1)} %fusion.29), kind=kOutput, calls=%fused_computation.47 | convolution fusion | flops 806354944 | bytes 8454144 | tf_op jit(solution)/shard_map/...cd,...ce->...de/dot_general | solution.py:27
  359.1 2.2 copy.60
  361.4 2.3 copy.59
  363.7 52.1 %while.47 = (s32[]{:T(128)}, f32[4,2,128,128]{3,2,1,0:T(8,128)S(1)}, f32[4,2,128,128]{3,2,1,0:T(8,128)}, f32[8,4,2,128,128]{4,3,2,1,0:T(8,128)}, f32[8,4,2,128,1...) while((s32[]{:T(128)}, ...), condition=%wide.region_3.4_spmd.clone, body=%wide.region_2.3_spmd.clone.sunk | while | flops 403046400 | bytes 7865975 | solution.py:94
  367.6 2.6 convolution_add_fusion.9
  374.1 2.6 convolution_add_fusion.9
  380.6 2.6 convolution_add_fusion.9
  387.2 2.6 convolution_add_fusion.9
  393.7 2.6 convolution_add_fusion.9
  400.2 2.6 convolution_add_fusion.9
  406.7 2.6 convolution_add_fusion.9
  413.2 2.6 convolution_add_fusion.9
  417.7 8.6 %while.48 = (s32[]{:T(128)}, f32[4,128,128]{2,1,0:T(8,128)S(1)}, f32[4,128,128]{2,1,0:T(8,128)}, f32[2,4,128,128]{3,2,1,0:T(8,128)}, f32[2,4,128,128]{3,2,1,0:T(...) while((s32[]{:T(128)}, f32[4,128,128]{2,1,0:T(8,128)S(1)}, ...), condition=%wide.region_5.6_spmd.clone, body=%wide.region_4.5_spmd.clone.sunk | while | flops 201523200 | bytes 3933815 | solution.py:101
  420.0 2.0 convolution_add_fusion.10
  424.3 2.0 convolution_add_fusion.10
  429.9 3.4 convolution_select_fusion
  433.4 3.0 fusion.43
  436.4 2.1 fusion.50
  438.5 43.8 %all-gather.8.cloned.1.call-done = f32[128,128,128]{2,1,0:T(8,128)} async-done(((f32[4,128,128]{2,1,0:T(8,128)}), f32[128,128,128]{2,1,0:T(8,128)}) %all-gather.8.cloned.1.call-update) | async-done | bytes 8388624 | tf_op jit(solution)/shard_map/all_gather | solution.py:15
  482.3 54.7 %all-gather.10.cloned.1.call-done = f32[128,128,128]{2,1,0:T(8,128)} async-done(((f32[4,128,128]{2,1,0:T(8,128)}), f32[128,128,128]{2,1,0:T(8,128)}) %all-gather.10.cloned.1.call-update) | async-done | bytes 8388624 | tf_op jit(solution)/shard_map/all_gather | solution.py:15
  537.0 46.1 %while.46 = (s32[]{:T(128)}, f32[4,128,128]{2,1,0:T(8,128)S(1)}, f32[4,128,128]{2,1,0:T(8,128)S(1)}, s32[]{:T(128)}, f32[32,4,128,128]{3,2,1,0:T(8,128)}, /*inde...) while((s32[]{:T(128)}, f32[4,128,128]{2,1,0:T(8,128)S(1)}, f32[4,128,128]{2,1,0:T(8,128)S(1)}, ...), condition=%wide.region_7.8_spmd, body=%wide.region_6.7_spmd.sunk | while | flops 201392128 | bytes 2884747 | solution.py:23
  584.2 6.3 bitcast_add_fusion
  590.5 3.9 fusion.59
  595.7 72.3 %all-gather.6.cloned.1.call-done = bf16[512,2048]{1,0:T(8,128)(2,1)} async-done(((bf16[512,512]{1,0:T(8,128)(2,1)}), bf16[512,2048]{1,0:T(8,128)(2,1)}) %all-gather.6.cloned.1.call-update) | async-done | bytes 2097168 | tf_op jit(solution)/shard_map/all_gather | solution.py:128
  668.1 4.3 fusion.56
  (159 shorter events, 92.2 us)
Async XLA Ops:
  6.5 576.6 %copy-start = (f32[4,128,128]{2,1,0:T(8,128)S(1)}, f32[4,128,128]{2,1,0:T(8,128)}, u32[]{:S(2)}) copy-start(f32[4,128,128]{2,1,0:T(8,128)} %param.14) | copy-start | bytes 786436
  6.5 475.7 %all-gather.8.cloned.1.call-start = ((), (), s32[]{:S(2)}) async-start(), calls=%async_computation.1 | async-start | bytes 8650752 | tf_op jit(solution)/shard_map/all_gather | solution.py:15
  7.3 5.6 copy-start.6
  9.4 1.3 copy-start.3
  14.9 3.2 copy-start.9
  345.4 13.7 %copy-start.1 = (f32[4,16,64,256]{3,2,1,0:T(8,128)}, f32[4,16,64,256]{3,2,1,0:T(8,128)S(1)}, u32[]{:S(2)}) copy-start(f32[4,16,64,256]{3,2,1,0:T(8,128)S(1)} %fusion.29) | copy-start | bytes 12582916
  426.3 0.7 copy-start.4
  427.1 109.9 %all-gather.10.cloned.1.call-start = ((), (), s32[]{:S(2)}) async-start(), calls=%async_computation.2 | async-start | bytes 8650752 | tf_op jit(solution)/shard_map/all_gather | solution.py:15
  427.8 240.2 %all-gather.6.cloned.1.call-start = ((), (), s32[]{:S(2)}) async-start(), calls=%async_computation | async-start | bytes 2621440 | tf_op jit(solution)/shard_map/all_gather | solution.py:128
  429.5 3.9 copy-start.2
  537.0 46.6 %copy-start.7 = (f32[2,4,128,128]{3,2,1,0:T(8,128)S(1)}, f32[2,4,128,128]{3,2,1,0:T(8,128)}, u32[]{:S(2)}) copy-start(f32[2,4,128,128]{3,2,1,0:T(8,128)} %get-tuple-element.122) | copy-start | bytes 1572868
  537.0 46.6 %copy-start.8 = (f32[2,4,128,128]{3,2,1,0:T(8,128)S(1)}, f32[2,4,128,128]{3,2,1,0:T(8,128)}, u32[]{:S(2)}) copy-start(f32[2,4,128,128]{3,2,1,0:T(8,128)} %get-tuple-element.127) | copy-start | bytes 1572868
  584.2 6.3 copy-start.5
Sparse Core Ops, SparseCore 0:
  427.2 55.0 all-gather.7
  484.5 52.3 all-gather.9
  595.8 72.1 all-gather.5
where the time goes:
time: 688 us; the launch traced here: 679 us
  other arithmetic  331 us (48%)
  waiting for transfers between devices  172 us (25%)
  matrix products  132 us (19%)
  local copies, waits for them, and re-layouts  29 us (4%)
  between operations  13.7 us (2%)
    another operation x4, other arithmetic, block_parts(): jax.scipy.linalg.solve_triangular(system, stacked, lower=True, unit_diago...  317 us
    dot_general x62, matrix products, product(): return jnp.einsum(pattern, left, right, precision=lax.Precision.HIGHEST)  122 us
    all_gather x2, waiting for transfers between devices, carried_in(): gathered = jax.tree.map(lambda a: lax.all_gather(a, axis), part)  98.5 us
    all_gather x1, waiting for transfers between devices, local(): lax.all_gather(attended, 'head', axis=1, tiled=True)  72.3 us
  transfers between devices with their start and end apart: 3, of which 3 were waited for; matrix products, arithmetic and copies ran while one was open for 2% of the time, Pallas kernels for 0%

commit v1 on v0

v1 whole, which is shorter than its diff:
```python
import jax
import jax.numpy as jnp
from jax import lax
from jax.sharding import PartitionSpec as P

HEAD_DIM = 128
BLOCK = 32


epsilon = 1e-06


def product(left, right, pattern):
    return jnp.einsum(pattern, left, right, precision=lax.Precision.HIGHEST)


def unit_rows(entries):
    return entries * lax.rsqrt(jnp.sum(entries * entries, axis=-1, keepdims=True) + epsilon)


def unit_lower_inverse(strict):
    size = strict.shape[-1]
    rows = lax.broadcasted_iota(jnp.int32, (size, size), 0)
    cols = lax.broadcasted_iota(jnp.int32, (size, size), 1)
    inverse = jnp.broadcast_to(jnp.eye(size, dtype=jnp.float32), strict.shape)
    width = 1
    while width < size:
        lower_left = (rows // (2 * width) == cols // (2 * width)) & (
            (rows // width) % 2 == 1
        ) & ((cols // width) % 2 == 0)
        coupling = jnp.where(lower_left, strict, 0.0)
        inverse = inverse - product(
            product(inverse, coupling, "...ij,...jk->...ik"), inverse, "...ij,...jk->...ik"
        )
        width *= 2
    return inverse


def block_parts(query_block, key_block, value_block):
    query_block = unit_rows(query_block.astype(jnp.float32))
    key_block = unit_rows(key_block.astype(jnp.float32))
    value_block = value_block.astype(jnp.float32)
    state_width = key_block.shape[-1]
    micro_len = key_block.shape[-2]
    gram = product(key_block, key_block, "...id,...jd->...ij")
    strict = jnp.tril(jnp.ones((micro_len, micro_len), jnp.float32), -1)
    inverse = unit_lower_inverse(2.0 * gram * strict)
    stacked = 2.0 * jnp.concatenate([key_block, value_block], axis=-1)
    solved = product(inverse, stacked, "...ij,...jk->...ik")
    writes = solved[..., :state_width]
    updates = solved[..., state_width:]
    scores = product(query_block, key_block, "...id,...jd->...ij")
    row_index = lax.broadcasted_iota(jnp.int32, (query_block.shape[-2], micro_len), 0)
    col_index = lax.broadcasted_iota(jnp.int32, (query_block.shape[-2], micro_len), 1)
    scores = jnp.where(col_index <= 2 * row_index + 1, scores, jnp.zeros_like(scores))
    adjusted = query_block - product(scores, writes, "...ij,...jd->...id")
    inside = product(scores, updates, "...ij,...jd->...id")
    moving = jnp.eye(state_width, dtype=jnp.float32) - product(
        key_block, writes, "...cd,...ce->...de"
    )
    carried = product(key_block, updates, "...cd,...ce->...de")
    return (adjusted, inside, moving, carried)


def compose(earlier, later):
    return (
        product(later[0], earlier[0], "...ij,...jk->...ik"),
        product(later[0], earlier[1], "...ij,...jk->...ik") + later[1],
    )


def block_prefix(moving, carried):
    count = moving.shape[1]
    identity = jnp.broadcast_to(jnp.eye(moving.shape[-1], dtype=jnp.float32), moving.shape)
    zeros = jnp.zeros_like(carried)
    shift = 1
    while shift < count:
        earlier = (
            jnp.concatenate([identity[:, :shift], moving[:, :-shift]], axis=1),
            jnp.concatenate([zeros[:, :shift], carried[:, :-shift]], axis=1),
        )
        moving, carried = compose(earlier, (moving, carried))
        shift *= 2
    return moving, carried


def shard_prefix(own, axis):
    count = lax.axis_size(axis)
    place = lax.axis_index(axis)
    span = own
    before = (
        jnp.broadcast_to(jnp.eye(own[0].shape[-1], dtype=jnp.float32), own[0].shape),
        jnp.zeros_like(own[1]),
    )
    shift = 1
    while shift < count:
        pairs = [(i, i + shift) for i in range(count - shift)]
        got = jax.tree.map(lambda a: lax.ppermute(a, axis, pairs), span)
        valid = place >= shift
        new_before = compose(got, before)
        before = jax.tree.map(lambda n, o: jnp.where(valid, n, o), new_before, before)
        if 2 * shift < count:
            new_span = compose(got, span)
            span = jax.tree.map(lambda n, o: jnp.where(valid, n, o), new_span, span)
        shift *= 2
    return before


def local(queries, key_pairs, value_pairs, init_state, out_weight):
    tokens = queries.shape[0]
    head_count = queries.shape[1] // HEAD_DIM
    blocks = tokens // BLOCK
    state_width = HEAD_DIM
    query_blocks = jnp.transpose(queries.reshape(blocks, BLOCK, head_count, HEAD_DIM), (2, 0, 1, 3))
    key_blocks = jnp.transpose(
        key_pairs.reshape(blocks, 2 * BLOCK, head_count, HEAD_DIM), (2, 0, 1, 3)
    )
    value_blocks = jnp.transpose(
        value_pairs.reshape(blocks, 2 * BLOCK, head_count, HEAD_DIM), (2, 0, 1, 3)
    )
    adjusted, inside, moving, carried = block_parts(query_blocks, key_blocks, value_blocks)
    prefix_move, prefix_carry = block_prefix(moving, carried)
    shard_map_pair = (prefix_move[:, -1], prefix_carry[:, -1])
    identity = jnp.broadcast_to(
        jnp.eye(state_width, dtype=jnp.float32), (head_count, 1, state_width, state_width)
    )
    start_move = jnp.concatenate([identity, prefix_move[:, :-1]], axis=1)
    start_carry = jnp.concatenate([jnp.zeros_like(identity), prefix_carry[:, :-1]], axis=1)
    query_part = product(adjusted, start_move, "hbcd,hbde->hbce")
    fixed_part = product(adjusted, start_carry, "hbcd,hbde->hbce") + inside
    before_move, before_carry = shard_prefix(shard_map_pair, "seq")
    entering = product(before_move, init_state, "hij,hjk->hik") + before_carry
    attended_heads = product(
        query_part.reshape(head_count, tokens, state_width), entering, "htd,hde->hte"
    ) + fixed_part.reshape(head_count, tokens, state_width)
    attended = (
        jnp.transpose(attended_heads, (1, 0, 2))
        .reshape(tokens, head_count * state_width)
        .astype(jnp.bfloat16)
    )
    groups = lax.axis_size("head")
    group = lax.axis_index("head")
    features = attended.shape[1]
    model_cols = out_weight.shape[1] // groups
    own_cols = lax.dynamic_slice_in_dim(out_weight, group * model_cols, model_cols, 1)

    def partial(block, source):
        rows = lax.dynamic_slice_in_dim(own_cols, source * features, features, 0)
        return jnp.dot(block, rows, preferred_element_type=jnp.float32)

    total = partial(attended, group)
    for offset in range(1, groups):
        pairs = [(i, (i + offset) % groups) for i in range(groups)]
        received = lax.ppermute(attended, "head", pairs)
        total = total + partial(received, (group - offset) % groups)
    return total.astype(jnp.bfloat16)


def solution(mesh):
    in_specs = (
        P("seq", "head"),
        P("seq", None, "head"),
        P("seq", None, "head"),
        P("head", None, None),
        P(),
    )
    out_specs = P("seq", "head")
    return jax.shard_map(local, mesh=mesh, in_specs=in_specs, out_specs=out_specs, check_vma=False)
```

time: 688 us -> 227 us (0.33)
  other arithmetic: 331 us -> 5.91 us
  waiting for transfers between devices: 172 us -> 35.5 us
  starting transfers between devices: 0.29 us -> 34.7 us
  between operations: 13.7 us -> 1.07 us
  local copies, waits for them, and re-layouts: 29 us -> 17.1 us
    another operation x8 -> x0, other arithmetic: 317 us -> none  [the longest x4 317 us: block_parts(): jax.scipy.linalg.solve_triangular(system, stacked, lower=True, unit_diago...]
    all_gather x3 -> x0, waiting for transfers between devices: 171 us -> none  [the longest x2 98.5 us: carried_in(): gathered = jax.tree.map(lambda a: lax.all_gather(a, axis), part)]
    ppermute x0 -> x13, waiting for transfers between devices: none -> 35.5 us  [the longest x10 25.1 us: shard_prefix(): got = jax.tree.map(lambda a: lax.ppermute(a, axis, pairs), span)]
    ppermute x0 -> x13, starting transfers between devices: none -> 34.7 us  [the longest x10 29.6 us: shard_prefix(): got = jax.tree.map(lambda a: lax.ppermute(a, axis, pairs), span)]
    while x54 -> x0, local copies, waits for them, and re-layouts: 13.1 us -> none
    dynamic_update_slice x10 -> x0, other arithmetic: 10.5 us -> none  [the longest x8 8.79 us: local(): lax.scan(advance_map, (group_identity, group_zeros), (grouped(moving), gr...]
    dot_general x62 -> x49, matrix products: 122 us -> 121 us  [product(): return jnp.einsum(pattern, left, right, precision=lax.Precision.HIGHEST)]
  transfers between devices with their start and end apart: 3 -> 13, of which waited for: 3 -> 8; matrix products, arithmetic and copies ran while one was open for 2% -> 29% of each run, Pallas kernels for 0% -> 0%
where the time goes in v1:
time: 227 us; the launch traced here: 223 us
  matrix products  129 us (57%)
  waiting for transfers between devices  35.5 us (16%)
  starting transfers between devices  34.7 us (15%)
  local copies, waits for them, and re-layouts  17.1 us (8%)
  other arithmetic  5.91 us (3%)
    dot_general x49, matrix products, product(): return jnp.einsum(pattern, left, right, precision=lax.Precision.HIGHEST)  121 us
    ppermute x10, starting transfers between devices, shard_prefix(): got = jax.tree.map(lambda a: lax.ppermute(a, axis, pairs), span)  29.6 us
    ppermute x10, waiting for transfers between devices, shard_prefix(): got = jax.tree.map(lambda a: lax.ppermute(a, axis, pairs), span)  25.1 us
    ppermute x3, waiting for transfers between devices, local(): received = lax.ppermute(attended, 'head', pairs)  10.4 us
    dot_general x4, matrix products, partial(): return jnp.dot(block, rows, preferred_element_type=jnp.float32)  7.77 us
    ppermute x3, starting transfers between devices, local(): received = lax.ppermute(attended, 'head', pairs)  5.05 us
  transfers between devices with their start and end apart: 13, of which 8 were waited for; matrix products, arithmetic and copies ran while one was open for 29% of the time, Pallas kernels for 0%

profile of v1, /device:TPU:16, one launch (start us, length us, event | category | flops | bytes accessed | tf_op | source)
XLA Modules:
  0.0 223.4 jit_solution(18138581004012717970)
XLA Ops:
  12.1 3.4 %convolution_multiply_fusion = f32[4,16,64,64]{3,2,1,0:T(8,128)S(1)} fusion(f32[4,16,64,128]{3,2,1,0:T(8,128)S(1)} %bitcast_multiply_fusion, f32[64,64]{1,0:T(8,128)S(1)} %select_multiply_fusion), kind=kOutput, calls=%fused_computation.72 | convolution fusion | flops 402915328 | bytes 3162112 | tf_op jit(solution)/shard_map/...id,...jd->...ij/dot_general | solution.py:14
  22.0 2.6 %convolution_subtract_fusion.4 = f32[4,16,64,64]{3,2,1,0:T(8,128)S(1)} fusion(f32[4,16,64,64]{3,2,1,0:T(8,128)S(1)} %fusion.63, f32[4,16,64,64]{3,2,1,0:T(8,128)S(1)} %fusion.103, f32[64,64]{1,0:T(8,128)S(1)} %fusion.161), kind=kOutput, calls=%fused_computation.69 | convolution fusion | flops 201850880 | bytes 3162112 | tf_op jit(solution)/shard_map/...ij,...jk->...ik/dot_general | solution.py:14
  26.9 2.4 %convolution_subtract_fusion.3 = f32[4,16,64,64]{3,2,1,0:T(8,128)S(1)} fusion(f32[4,16,64,64]{3,2,1,0:T(8,128)S(1)} %convolution_subtract_fusion.4, f32[4,16,64,64]{3,2,1,0:T(8,128)S(1)} %fusion.61), kind=kOutput, calls=%fused_computation.68 | convolution fusion | flops 201588736 | bytes 3145728 | tf_op jit(solution)/shard_map/...ij,...jk->...ik/dot_general | solution.py:14
  31.6 2.4 %convolution_subtract_fusion.2 = f32[4,16,64,64]{3,2,1,0:T(8,128)S(1)} fusion(f32[4,16,64,64]{3,2,1,0:T(8,128)S(1)} %convolution_subtract_fusion.3, f32[4,16,64,64]{3,2,1,0:T(8,128)S(1)} %fusion.59), kind=kOutput, calls=%fused_computation.67 | convolution fusion | flops 201588736 | bytes 3145728 | tf_op jit(solution)/shard_map/...ij,...jk->...ik/dot_general | solution.py:14
  36.3 2.8 %convolution_subtract_fusion.1 = f32[4,16,64,64]{3,2,1,0:T(8,128)S(1)} fusion(f32[4,16,64,64]{3,2,1,0:T(8,128)S(1)} %convolution_subtract_fusion.2, f32[4,16,64,64]{3,2,1,0:T(8,128)S(1)} %fusion.57), kind=kOutput, calls=%fused_computation.66 | convolution fusion | flops 201588736 | bytes 3145728 | tf_op jit(solution)/shard_map/...ij,...jk->...ik/dot_general | solution.py:14
  43.7 4.0 %fusion.2 = f32[4,16,64,256]{3,2,1,0:T(8,128)S(1)} fusion(f32[4,16,64,128]{3,2,1,0:T(8,128)S(1)} %bitcast.99, f32[4,16,64,128]{3,2,1,0:T(8,128)S(1)} %bitcast_multiply_fusion, f32[4,16,64,64]{3,2,1,0:T(8,128)S(1)} %convolution_subtract_fusion.1, f32[4,16,64,64]{3,2,1,0:T(8,128)S(1)} %fusion.183), kind=kOutput, calls=%fused_computation.5 | convolution fusion | flops 807665664 | bytes 10485760 | tf_op jit(solution)/shard_map/...ij,...jk->...ik/dot_general | solution.py:14
  47.8 6.9 %convolution_subtract_fusion = f32[4,16,128,128]{3,2,1,0:T(8,128)S(1)} fusion(f32[4,16,64,128]{3,2,1,0:T(8,128)S(1)} %bitcast_multiply_fusion, f32[128,128]{1,0:T(8,128)S(1)} %fusion.122, f32[4,16,64,256]{3,2,1,0:T(8,128)S(1)} %fusion.2), kind=kOutput, calls=%fused_computation.40 | convolution fusion | flops 806354944 | bytes 8454144 | tf_op jit(solution)/shard_map/...cd,...ce->...de/dot_general | solution.py:14
  55.2 4.7 %fusion.1 = f32[4,16,128,128]{3,2,1,0:T(8,128)S(1)} fusion(f32[4,16,128,128]{3,2,1,0:T(8,128)S(1)} %convolution_subtract_fusion, f32[4,1,128,128]{3,2,1,0:T(8,128)S(1)} %broadcast_in_dim.81, f32[4,15,128,128]{3,2,1,0:T(8,128)S(1)} %slice.73), kind=kOutput, calls=%fused_computation.3 | convolution fusion | flops 1611661312 | bytes 12582912 | tf_op jit(solution)/shard_map/...ij,...jk->...ik/dot_general | solution.py:14
  60.4 4.9 %fusion.6 = f32[4,16,128,128]{3,2,1,0:T(8,128)S(1)} fusion(f32[4,16,128,128]{3,2,1,0:T(8,128)S(1)} %fusion.1, f32[4,14,128,128]{3,2,1,0:T(8,128)S(1)} %slice.74, f32[4,2,128,128]{3,2,1,0:T(8,128)S(1)} %slice.57), kind=kOutput, calls=%fused_computation.9 | convolution fusion | flops 1611661312 | bytes 12582912 | tf_op jit(solution)/shard_map/...ij,...jk->...ik/dot_general | solution.py:14
  65.8 4.9 %fusion.10 = f32[4,16,128,128]{3,2,1,0:T(8,128)S(1)} fusion(f32[4,16,128,128]{3,2,1,0:T(8,128)S(1)} %fusion.6, f32[4,12,128,128]{3,2,1,0:T(8,128)S(1)} %slice.75, f32[4,4,128,128]{3,2,1,0:T(8,128)S(1)} %slice.59), kind=kOutput, calls=%fused_computation.13 | convolution fusion | flops 1611661312 | bytes 12582912 | tf_op jit(solution)/shard_map/...ij,...jk->...ik/dot_general | solution.py:14
  72.5 7.3 %fusion.14 = f32[4,16,128,128]{3,2,1,0:T(8,128)} fusion(f32[4,16,128,128]{3,2,1,0:T(8,128)S(1)} %fusion.10, f32[4,8,128,128]{3,2,1,0:T(8,128)S(1)} %slice.76, f32[4,8,128,128]{3,2,1,0:T(8,128)} %slice.61), kind=kOutput, calls=%fused_computation.17 | convolution fusion | flops 1611661312 | bytes 12582912 | tf_op jit(solution)/shard_map/...ij,...jk->...ik/dot_general | solution.py:14
  83.4 8.4 %fusion.69 = f32[4,16,128,128]{3,2,1,0:T(8,128)} fusion(f32[4,16,64,128]{3,2,1,0:T(8,128)S(1)} %bitcast_multiply_fusion, f32[4,16,64,256]{3,2,1,0:T(8,128)S(1)} %fusion.2), kind=kOutput, calls=%fused_computation.61 | convolution fusion | flops 805306368 | bytes 8388608 | tf_op jit(solution)/shard_map/...cd,...ce->...de/dot_general | solution.py:14
  91.7 6.7 %copy_add_fusion = f32[4,16,128,128]{3,2,0,1:T(8,128)S(1)} fusion(f32[4,16,128,128]{3,2,1,0:T(8,128)} %fusion.69, f32[4,16,128,128]{3,2,1,0:T(8,128)S(1)} %convolution_subtract_fusion), kind=kOutput, calls=%fused_computation.33 | convolution fusion | flops 1611661312 | bytes 16515072 | tf_op jit(solution)/shard_map/...ij,...jk->...ik/dot_general | solution.py:14
  98.8 4.5 %fusion.33 = f32[4,16,128,128]{3,2,0,1:T(8,128)S(1)} fusion(f32[4,16,128,128]{3,2,0,1:T(8,128)S(1)} %copy_add_fusion, f32[4,14,128,128]{3,2,0,1:T(8,128)S(1)} %slice.81, f32[4,16,128,128]{3,2,1,0:T(8,128)S(1)} %fusion.1), kind=kOutput, calls=%fused_computation.37 | convolution fusion | flops 1611661312 | bytes 16252928 | tf_op jit(solution)/shard_map/...ij,...jk->...ik/dot_general | solution.py:14
  103.7 4.4 %fusion.38 = f32[4,16,128,128]{3,2,0,1:T(8,128)S(1)} fusion(f32[4,16,128,128]{3,2,0,1:T(8,128)S(1)} %fusion.33, f32[4,12,128,128]{3,2,0,1:T(8,128)S(1)} %slice.82, f32[4,16,128,128]{3,2,1,0:T(8,128)S(1)} %fusion.6), kind=kOutput, calls=%fused_computation.38 | convolution fusion | flops 1611661312 | bytes 15728640 | tf_op jit(solution)/shard_map/...ij,...jk->...ik/dot_general | solution.py:14
  108.4 4.3 %fusion.43 = f32[4,16,128,128]{3,2,0,1:T(8,128)S(1)} fusion(f32[4,16,128,128]{3,2,0,1:T(8,128)S(1)} %fusion.38, f32[4,8,128,128]{3,2,0,1:T(8,128)S(1)} %slice.83, f32[4,16,128,128]{3,2,1,0:T(8,128)S(1)} %fusion.10), kind=kOutput, calls=%fused_computation.39 | convolution fusion | flops 1611661312 | bytes 14680064 | tf_op jit(solution)/shard_map/...ij,...jk->...ik/dot_general | solution.py:14
  115.4 3.9 %collective-permute-start.5 = (f32[4,128,128]{2,1,0:T(8,128)}, f32[4,128,128]{2,1,0:T(8,128)}, u32[]{:S(2)}, u32[]{:S(2)}) collective-permute-start(f32[4,128,128]{2,1,0:T(8,128)} %slice_bitcast_fusion), channel_id=1, source_target_pairs={{0,4},{4,8},{8,12},{12,16},{16,20},{20,24},{24,28},{28,32},{32,36}... | collective-permute-start | bytes 786440 | tf_op jit(solution)/shard_map/ppermute | solution.py:98
  121.2 3.4 %convolution_select_fusion = f32[4,16,32,64]{3,2,1,0:T(8,128)S(1)} fusion(f32[4,16,64,128]{3,2,1,0:T(8,128)S(1)} %bitcast_multiply_fusion, f32[16,32,4,128]{3,2,1,0:T(4,128)S(1)} %reshape.56, f32[4,16,32]{2,1,0:T(8,128)S(1)} %add_rsqrt_fusion.1, pred[32,64]{1,0:T(8,128)(4,1)S(1)} %iota_compare_fusion.3), kind=kOutput, calls=%fused_computation.73 | convolution fusion | flops 201719808 | bytes 3680256 | tf_op jit(solution)/shard_map/...id,...jd->...ij/dot_general | solution.py:14
  126.8 3.7 %fusion.19 = f32[4,16,32,128]{3,2,1,0:T(8,128)S(1)} fusion(f32[4,16,32,128]{3,2,1,0:T(8,128)S(1)} %fusion.76, f32[4,16,128,128]{3,2,0,1:T(8,128)S(1)} %copy-done.5), kind=kOutput, calls=%fused_computation.22 | convolution fusion | flops 402653184 | bytes 6029312 | tf_op jit(solution)/shard_map/hbcd,hbde->hbce/dot_general | solution.py:14
  132.7 4.2 %fusion = f32[4,16,32,128]{3,2,1,0:T(8,128)S(1)} fusion(f32[4,16,32,128]{3,2,1,0:T(8,128)S(1)} %fusion.76, f32[4,1,128,128]{3,2,1,0:T(8,128)S(1)} %copy-done.7, f32[4,15,128,128]{3,2,1,0:T(8,128)S(1)} %slice-done), kind=kOutput, calls=%fused_computation.2 | convolution fusion | flops 403701760 | bytes 6291456 | tf_op jit(solution)/shard_map/hbcd,hbde->hbce/dot_general | solution.py:14
  138.8 3.8 %collective-permute-start.1 = (f32[4,128,128]{2,1,0:T(8,128)S(1)}, f32[4,128,128]{2,1,0:T(8,128)S(1)}, u32[]{:S(2)}, u32[]{:S(2)}) collective-permute-start(f32[4,128,128]{2,1,0:T(8,128)S(1)} %convolution_select_fusion.8), channel_id=1, source_target_pairs={{0,8},{4,12},{8,16},{12,20},{16,24},{20,28},{24,32},{28,36},{32,40... | collective-permute-start | bytes 786440 | tf_op jit(solution)/shard_map/ppermute | solution.py:98
  144.2 3.5 %collective-permute-start.6 = (f32[4,128,128]{2,1,0:T(8,128)S(1)}, f32[4,128,128]{2,1,0:T(8,128)S(1)}, u32[]{:S(2)}, u32[]{:S(2)}) collective-permute-start(f32[4,128,128]{2,1,0:T(8,128)S(1)} %fusion.93), channel_id=1, source_target_pairs={{0,8},{4,12},{8,16},{12,20},{16,24},{20,28},{24,32},{28,36},{32,40... | collective-permute-start | bytes 786440 | tf_op jit(solution)/shard_map/ppermute | solution.py:98
  152.0 3.8 %collective-permute-start.2 = (f32[4,128,128]{2,1,0:T(8,128)S(1)}, f32[4,128,128]{2,1,0:T(8,128)S(1)}, u32[]{:S(2)}, u32[]{:S(2)}) collective-permute-start(f32[4,128,128]{2,1,0:T(8,128)S(1)} %convolution_select_fusion.6), channel_id=1, source_target_pairs={{0,16},{4,20},{8,24},{12,28},{16,32},{20,36},{24,40},{28,44},{32,4... | collective-permute-start | bytes 786440 | tf_op jit(solution)/shard_map/ppermute | solution.py:98
  157.1 3.4 %collective-permute-start.7 = (f32[4,128,128]{2,1,0:T(8,128)S(1)}, f32[4,128,128]{2,1,0:T(8,128)S(1)}, u32[]{:S(2)}, u32[]{:S(2)}) collective-permute-start(f32[4,128,128]{2,1,0:T(8,128)S(1)} %fusion.92), channel_id=1, source_target_pairs={{0,16},{4,20},{8,24},{12,28},{16,32},{20,36},{24,40},{28,44},{32,4... | collective-permute-start | bytes 786440 | tf_op jit(solution)/shard_map/ppermute | solution.py:98
  163.5 3.2 %collective-permute-start.3 = (f32[4,128,128]{2,1,0:T(8,128)S(1)}, f32[4,128,128]{2,1,0:T(8,128)S(1)}, u32[]{:S(2)}, u32[]{:S(2)}) collective-permute-start(f32[4,128,128]{2,1,0:T(8,128)S(1)} %convolution_select_fusion.4), channel_id=1, source_target_pairs={{0,32},{4,36},{8,40},{12,44},{16,48},{20,52},{24,56},{28,60},{32,6... | collective-permute-start | bytes 786440 | tf_op jit(solution)/shard_map/ppermute | solution.py:98
  166.7 3.7 %collective-permute-done.7 = f32[4,128,128]{2,1,0:T(8,128)S(1)} collective-permute-done((f32[4,128,128]{2,1,0:T(8,128)S(1)}, f32[4,128,128]{2,1,0:T(8,128)S(1)}, u32[]{:S(2)}, u32[]{:S(2)}) %collective-permute-start.7) | collective-permute-done | bytes 262176 | tf_op jit(solution)/shard_map/ppermute | solution.py:98
  170.9 3.3 %collective-permute-start.8 = (f32[4,128,128]{2,1,0:T(8,128)S(1)}, f32[4,128,128]{2,1,0:T(8,128)S(1)}, u32[]{:S(2)}, u32[]{:S(2)}) collective-permute-start(f32[4,128,128]{2,1,0:T(8,128)S(1)} %fusion.91), channel_id=1, source_target_pairs={{0,32},{4,36},{8,40},{12,44},{16,48},{20,52},{24,56},{28,60},{32,6... | collective-permute-start | bytes 786440 | tf_op jit(solution)/shard_map/ppermute | solution.py:98
  176.7 10.8 %collective-permute-done.8 = f32[4,128,128]{2,1,0:T(8,128)S(1)} collective-permute-done((f32[4,128,128]{2,1,0:T(8,128)S(1)}, f32[4,128,128]{2,1,0:T(8,128)S(1)}, u32[]{:S(2)}, u32[]{:S(2)}) %collective-permute-start.8) | collective-permute-done | bytes 262176 | tf_op jit(solution)/shard_map/ppermute | solution.py:98
  191.1 6.7 %collective-permute-done.9 = f32[4,128,128]{2,1,0:T(8,128)S(1)} collective-permute-done((f32[4,128,128]{2,1,0:T(8,128)S(1)}, f32[4,128,128]{2,1,0:T(8,128)S(1)}, u32[]{:S(2)}, u32[]{:S(2)}) %collective-permute-start.9) | collective-permute-done | bytes 262176 | tf_op jit(solution)/shard_map/ppermute | solution.py:98
  200.0 2.8 %collective-permute-start.12 = (bf16[512,512]{0,1:T(8,128)(2,1)}, bf16[512,512]{0,1:T(8,128)(2,1)S(1)}, u32[]{:S(2)}, u32[]{:S(2)}) collective-permute-start(bf16[512,512]{0,1:T(8,128)(2,1)} %bitcast.8), channel_id=1, source_target_pairs={{0,3},{1,0},{2,1},{3,2},{4,7},{5,4},{6,5},{7,6},{8,11},{9,8},{10,9... | collective-permute-start | bytes 1572872 | tf_op jit(solution)/shard_map/ppermute | solution.py:154
  206.9 8.5 %collective-permute-done.12 = bf16[512,512]{0,1:T(8,128)(2,1)S(1)} collective-permute-done((bf16[512,512]{0,1:T(8,128)(2,1)}, bf16[512,512]{0,1:T(8,128)(2,1)S(1)}, u32[]{:S(2)}, u32[]{:S(2)}) %collective-permute-start.12) | collective-permute-done | bytes 524320 | tf_op jit(solution)/shard_map/ppermute | solution.py:154
  220.7 2.5 %fusion.83 = bf16[512,512]{1,0:T(8,128)(2,1)} fusion(f32[512,512]{1,0:T(8,128)S(1)} %fusion.113, f32[512,512]{1,0:T(8,128)S(1)} %convolution_add_fusion.1, bf16[512,512]{0,1:T(8,128)(2,1)S(1)} %collective-permute-done.11, bf16[2048,2048]{1,0:T(8,128)(2,1)} %param.9, s32[]{:T(128)S(6)} %select_n.333, s32[]{:T(128)S(6)} %select_n.327), kind=kOutput, calls=%fused_computation.80 | convolution fusion | flops 269221888 | bytes 3670024 | tf_op jit(solution)/shard_map/dot_general | solution.py:149
  (120 shorter events, 76.3 us)
Async XLA Ops:
  0.0 190.7 %copy-start = (f32[4,128,128]{2,1,0:T(8,128)S(1)}, f32[4,128,128]{2,1,0:T(8,128)}, u32[]{:S(2)}) copy-start(f32[4,128,128]{2,1,0:T(8,128)} %param.8) | copy-start | bytes 786436
  4.4 1.3 copy-start.3
  5.7 2.2 %copy-start.8 = (bf16[512,2,512]{2,1,0:T(2,128)(2,1)S(1)}, bf16[512,2,512]{2,1,0:T(2,128)(2,1)}, u32[]{:S(2)}) copy-start(bf16[512,2,512]{2,1,0:T(2,128)(2,1)} %param.7) | copy-start | bytes 3145732
  10.1 1.9 copy-start.15
  12.0 3.5 %copy-start.9 = (s32[64]{0:T(128)S(1)}, s32[64]{0:T(128)}, u32[]{:S(2)}) copy-start(s32[64]{0:T(128)} %get-tuple-element.21) | copy-start | bytes 772
  12.0 3.5 %copy-start.10 = (s32[64]{0:T(128)S(1)}, s32[64]{0:T(128)}, u32[]{:S(2)}) copy-start(s32[64]{0:T(128)} %get-tuple-element.22) | copy-start | bytes 772
  12.1 3.5 %copy-start.11 = (s32[64]{0:T(128)S(1)}, s32[64]{0:T(128)}, u32[]{:S(2)}) copy-start(s32[64]{0:T(128)} %get-tuple-element.27) | copy-start | bytes 772
  12.1 3.5 %copy-start.12 = (s32[64]{0:T(128)S(1)}, s32[64]{0:T(128)}, u32[]{:S(2)}) copy-start(s32[64]{0:T(128)} %get-tuple-element.28) | copy-start | bytes 772
  12.1 3.5 %copy-start.13 = (pred[64]{0:T(512)(128)(4,1)S(1)}, pred[64]{0:T(512)(128)(4,1)}, u32[]{:S(2)}) copy-start(pred[64]{0:T(512)(128)(4,1)} %get-tuple-element.15) | copy-start | bytes 196
  12.1 3.5 %copy-start.14 = (pred[64]{0:T(512)(128)(4,1)S(1)}, pred[64]{0:T(512)(128)(4,1)}, u32[]{:S(2)}) copy-start(pred[64]{0:T(512)(128)(4,1)} %get-tuple-element.16) | copy-start | bytes 196
  47.8 35.6 %copy-start.1 = (f32[4,16,64,256]{3,2,1,0:T(8,128)}, f32[4,16,64,256]{3,2,1,0:T(8,128)S(1)}, u32[]{:S(2)}) copy-start(f32[4,16,64,256]{3,2,1,0:T(8,128)S(1)} %fusion.2) | copy-start | bytes 12582916
  55.2 4.7 %copy-start.6 = (f32[4,1,128,128]{3,2,1,0:T(8,128)}, f32[4,1,128,128]{3,2,1,0:T(8,128)S(1)}, u32[]{:S(2)}) copy-start(f32[4,1,128,128]{3,2,1,0:T(8,128)S(1)} %broadcast_in_dim.81) | copy-start | bytes 786436
  81.4 55.9 %collective-permute-start = (f32[4,128,128]{2,1,0:T(8,128)}, f32[4,128,128]{2,1,0:T(8,128)}, u32[]{:S(2)}, u32[]{:S(2)}) collective-permute-start(f32[4,128,128]{2,1,0:T(8,128)} %slice_bitcast_fusion.1), channel_id=1, source_target_pairs={{0,4},{4,8},{8,12},{12,16},{16,20},{20,24},{24,28},{28,32},{32,36}... | collective-permute-start | bytes 786440 | tf_op jit(solution)/shard_map/ppermute | solution.py:98
  112.7 2.0 copy-start.4
  115.4 27.2 %collective-permute-start.5 = (f32[4,128,128]{2,1,0:T(8,128)}, f32[4,128,128]{2,1,0:T(8,128)}, u32[]{:S(2)}, u32[]{:S(2)}) collective-permute-start(f32[4,128,128]{2,1,0:T(8,128)} %slice_bitcast_fusion), channel_id=1, source_target_pairs={{0,4},{4,8},{8,12},{12,16},{16,20},{20,24},{24,28},{28,32},{32,36}... | collective-permute-start | bytes 786440 | tf_op jit(solution)/shard_map/ppermute | solution.py:98
  121.2 3.4 %copy-start.2 = (f32[4,16,64,256]{3,2,1,0:T(8,128)S(1)}, f32[4,16,64,256]{3,2,1,0:T(8,128)}, u32[]{:S(2)}) copy-start(f32[4,16,64,256]{3,2,1,0:T(8,128)} %copy-done.1) | copy-start | bytes 12582916
  124.6 2.2 copy-start.5
  130.5 2.2 slice-start
  130.5 2.2 copy-start.7
  138.8 12.8 %collective-permute-start.1 = (f32[4,128,128]{2,1,0:T(8,128)S(1)}, f32[4,128,128]{2,1,0:T(8,128)S(1)}, u32[]{:S(2)}, u32[]{:S(2)}) collective-permute-start(f32[4,128,128]{2,1,0:T(8,128)S(1)} %convolution_select_fusion.8), channel_id=1, source_target_pairs={{0,8},{4,12},{8,16},{12,20},{16,24},{20,28},{24,32},{28,36},{32,40... | collective-permute-start | bytes 786440 | tf_op jit(solution)/shard_map/ppermute | solution.py:98
  144.2 12.5 %collective-permute-start.6 = (f32[4,128,128]{2,1,0:T(8,128)S(1)}, f32[4,128,128]{2,1,0:T(8,128)S(1)}, u32[]{:S(2)}, u32[]{:S(2)}) collective-permute-start(f32[4,128,128]{2,1,0:T(8,128)S(1)} %fusion.93), channel_id=1, source_target_pairs={{0,8},{4,12},{8,16},{12,20},{16,24},{20,28},{24,32},{28,36},{32,40... | collective-permute-start | bytes 786440 | tf_op jit(solution)/shard_map/ppermute | solution.py:98
  152.0 11.1 %collective-permute-start.2 = (f32[4,128,128]{2,1,0:T(8,128)S(1)}, f32[4,128,128]{2,1,0:T(8,128)S(1)}, u32[]{:S(2)}, u32[]{:S(2)}) collective-permute-start(f32[4,128,128]{2,1,0:T(8,128)S(1)} %convolution_select_fusion.6), channel_id=1, source_target_pairs={{0,16},{4,20},{8,24},{12,28},{16,32},{20,36},{24,40},{28,44},{32,4... | collective-permute-start | bytes 786440 | tf_op jit(solution)/shard_map/ppermute | solution.py:98
  157.1 13.3 %collective-permute-start.7 = (f32[4,128,128]{2,1,0:T(8,128)S(1)}, f32[4,128,128]{2,1,0:T(8,128)S(1)}, u32[]{:S(2)}, u32[]{:S(2)}) collective-permute-start(f32[4,128,128]{2,1,0:T(8,128)S(1)} %fusion.92), channel_id=1, source_target_pairs={{0,16},{4,20},{8,24},{12,28},{16,32},{20,36},{24,40},{28,44},{32,4... | collective-permute-start | bytes 786440 | tf_op jit(solution)/shard_map/ppermute | solution.py:98
  163.5 11.5 %collective-permute-start.3 = (f32[4,128,128]{2,1,0:T(8,128)S(1)}, f32[4,128,128]{2,1,0:T(8,128)S(1)}, u32[]{:S(2)}, u32[]{:S(2)}) collective-permute-start(f32[4,128,128]{2,1,0:T(8,128)S(1)} %convolution_select_fusion.4), channel_id=1, source_target_pairs={{0,32},{4,36},{8,40},{12,44},{16,48},{20,52},{24,56},{28,60},{32,6... | collective-permute-start | bytes 786440 | tf_op jit(solution)/shard_map/ppermute | solution.py:98
  170.9 16.7 %collective-permute-start.8 = (f32[4,128,128]{2,1,0:T(8,128)S(1)}, f32[4,128,128]{2,1,0:T(8,128)S(1)}, u32[]{:S(2)}, u32[]{:S(2)}) collective-permute-start(f32[4,128,128]{2,1,0:T(8,128)S(1)} %fusion.91), channel_id=1, source_target_pairs={{0,32},{4,36},{8,40},{12,44},{16,48},{20,52},{24,56},{28,60},{32,6... | collective-permute-start | bytes 786440 | tf_op jit(solution)/shard_map/ppermute | solution.py:98
  175.4 14.8 %collective-permute-start.4 = (f32[4,128,128]{2,1,0:T(8,128)S(1)}, f32[4,128,128]{2,1,0:T(8,128)S(1)}, u32[]{:S(2)}, u32[]{:S(2)}) collective-permute-start(f32[4,128,128]{2,1,0:T(8,128)S(1)} %convolution_select_fusion.2), channel_id=1, source_target_pairs={{0,64},{4,68},{8,72},{12,76},{16,80},{20,84},{24,88},{28,92},{32,9... | collective-permute-start | bytes 786440 | tf_op jit(solution)/shard_map/ppermute | solution.py:98
  188.0 9.8 %collective-permute-start.9 = (f32[4,128,128]{2,1,0:T(8,128)S(1)}, f32[4,128,128]{2,1,0:T(8,128)S(1)}, u32[]{:S(2)}, u32[]{:S(2)}) collective-permute-start(f32[4,128,128]{2,1,0:T(8,128)S(1)} %fusion.90), channel_id=1, source_target_pairs={{0,64},{4,68},{8,72},{12,76},{16,80},{20,84},{24,88},{28,92},{32,9... | collective-permute-start | bytes 786440 | tf_op jit(solution)/shard_map/ppermute | solution.py:98
  200.0 15.4 %collective-permute-start.12 = (bf16[512,512]{0,1:T(8,128)(2,1)}, bf16[512,512]{0,1:T(8,128)(2,1)S(1)}, u32[]{:S(2)}, u32[]{:S(2)}) collective-permute-start(bf16[512,512]{0,1:T(8,128)(2,1)} %bitcast.8), channel_id=1, source_target_pairs={{0,3},{1,0},{2,1},{3,2},{4,7},{5,4},{6,5},{7,6},{8,11},{9,8},{10,9... | collective-permute-start | bytes 1572872 | tf_op jit(solution)/shard_map/ppermute | solution.py:154
  202.8 16.2 %collective-permute-start.10 = (bf16[512,512]{0,1:T(8,128)(2,1)}, bf16[512,512]{0,1:T(8,128)(2,1)S(1)}, u32[]{:S(2)}, u32[]{:S(2)}) collective-permute-start(bf16[512,512]{0,1:T(8,128)(2,1)} %bitcast.8), channel_id=1, source_target_pairs={{0,1},{1,2},{2,3},{3,0},{4,5},{5,6},{6,7},{7,4},{8,9},{9,10},{10,1... | collective-permute-start | bytes 1572872 | tf_op jit(solution)/shard_map/ppermute | solution.py:154
  202.8 17.9 %collective-permute-start.11 = (bf16[512,512]{0,1:T(8,128)(2,1)}, bf16[512,512]{0,1:T(8,128)(2,1)S(1)}, u32[]{:S(2)}, u32[]{:S(2)}) collective-permute-start(bf16[512,512]{0,1:T(8,128)(2,1)} %bitcast.8), channel_id=1, source_target_pairs={{0,2},{1,3},{2,0},{3,1},{4,6},{5,7},{6,4},{7,5},{8,10},{9,11},{10,... | collective-permute-start | bytes 1572872 | tf_op jit(solution)/shard_map/ppermute | solution.py:154

commit v2 on v1

--- a/solution.py
+++ b/solution.py
@@ -95,7 +95,9 @@
     shift = 1
     while shift < count:
         pairs = [(i, i + shift) for i in range(count - shift)]
-        got = jax.tree.map(lambda a: lax.ppermute(a, axis, pairs), span)
+        packed = lax.ppermute(jnp.concatenate(span, axis=-1), axis, pairs)
+        width = span[0].shape[-1]
+        got = (packed[..., :width], packed[..., width:])
         valid = place >= shift
         new_before = compose(got, before)
         before = jax.tree.map(lambda n, o: jnp.where(valid, n, o), new_before, before)

time: 227 us -> 285 us (1.26)
  the two profiles are of different devices: /device:TPU:16 before, /device:TPU:48 now
where the time goes in v2:
time: 285 us; the launch traced here: 281 us
  matrix products  169 us (59%)
  waiting for transfers between devices  43.9 us (15%)
  local copies, waits for them, and re-layouts  37.8 us (13%)
  starting transfers between devices  21.1 us (7%)
  other arithmetic  8.49 us (3%)
    dot_general x49, matrix products, product(): return jnp.einsum(pattern, left, right, precision=lax.Precision.HIGHEST)  161 us
    ppermute x5, waiting for transfers between devices, shard_prefix(): packed = lax.ppermute(jnp.concatenate(span, axis=-1), axis, pairs)  25.5 us
    unnamed x73, local copies, waits for them, and re-layouts  18.8 us
    ppermute x3, waiting for transfers between devices, local(): received = lax.ppermute(attended, 'head', pairs)  18.4 us
    ppermute x5, starting transfers between devices, shard_prefix(): packed = lax.ppermute(jnp.concatenate(span, axis=-1), axis, pairs)  15.8 us
    dot_general x4, matrix products, partial(): return jnp.dot(block, rows, preferred_element_type=jnp.float32)  7.62 us
    slice x8, local copies, waits for them, and re-layouts, block_prefix(): moving[:, :-shift]  6.88 us
  transfers between devices with their start and end apart: 8, of which 6 were waited for; matrix products, arithmetic and copies ran while one was open for 15% of the time, Pallas kernels for 0%

profile of v2, /device:TPU:48, one launch (start us, length us, event | category | flops | bytes accessed | tf_op | source)
XLA Modules:
  0.0 281.3 jit_solution(3300601646790667075)
XLA Ops:
  7.9 2.5 reshape.58
  12.4 3.4 %convolution_multiply_fusion = f32[4,16,64,64]{3,2,1,0:T(8,128)S(1)} fusion(f32[4,16,64,128]{3,2,1,0:T(8,128)S(1)} %bitcast_multiply_fusion, f32[64,64]{1,0:T(8,128)S(1)} %select_multiply_fusion), kind=kOutput, calls=%fused_computation.74 | convolution fusion | flops 402915328 | bytes 3162112 | tf_op jit(solution)/shard_map/...id,...jd->...ij/dot_general | solution.py:14
  20.0 2.3 fusion.67
  22.4 2.6 convolution_subtract_fusion.4
  27.2 2.4 convolution_subtract_fusion.3
  31.9 2.4 convolution_subtract_fusion.2
  36.6 2.6 convolution_subtract_fusion.1
  43.8 4.4 %fusion = f32[4,16,64,256]{3,2,1,0:T(8,128)S(1)} fusion(f32[4,16,64,128]{3,2,1,0:T(8,128)S(1)} %bitcast.81, f32[4,16,64,128]{3,2,1,0:T(8,128)S(1)} %bitcast_multiply_fusion, f32[4,16,64,64]{3,2,1,0:T(8,128)S(1)} %convolution_subtract_fusion.1, f32[4,16,64,64]{3,2,1,0:T(8,128)S(1)} %fusion.205), kind=kOutput, calls=%fused_computation.1 | convolution fusion | flops 807665664 | bytes 10485760 | tf_op jit(solution)/shard_map/...ij,...jk->...ik/dot_general | solution.py:14
  48.2 7.3 %fusion.73 = f32[4,16,128,128]{2,3,1,0:T(8,128)S(1)} fusion(f32[4,16,64,128]{3,2,1,0:T(8,128)S(1)} %bitcast_multiply_fusion, f32[4,16,64,256]{3,2,1,0:T(8,128)S(1)} %fusion), kind=kOutput, calls=%fused_computation.63 | convolution fusion | flops 805306368 | bytes 8388608 | tf_op jit(solution)/shard_map/...cd,...ce->...de/dot_general | solution.py:14
  55.6 7.0 %convolution_subtract_fusion = f32[4,16,128,128]{3,2,1,0:T(8,128)S(1)} fusion(f32[4,16,64,128]{3,2,1,0:T(8,128)S(1)} %bitcast_multiply_fusion, f32[128,128]{1,0:T(8,128)S(1)} %fusion.144, f32[4,16,64,256]{3,2,1,0:T(8,128)S(1)} %fusion), kind=kOutput, calls=%fused_computation.42 | convolution fusion | flops 806354944 | bytes 8454144 | tf_op jit(solution)/shard_map/...cd,...ce->...de/dot_general | solution.py:14
  64.6 9.2 %copy_add_fusion = f32[4,16,128,128]{2,3,0,1:T(8,128)S(1)} fusion(f32[4,16,128,128]{2,3,1,0:T(8,128)S(1)} %fusion.73, f32[4,16,128,128]{3,2,1,0:T(8,128)S(1)} %convolution_subtract_fusion), kind=kOutput, calls=%fused_computation.35 | convolution fusion | flops 1611661312 | bytes 16515072 | tf_op jit(solution)/shard_map/...ij,...jk->...ik/dot_general | solution.py:14
  77.5 6.8 %fusion.3 = f32[4,16,128,128]{3,2,1,0:T(8,128)S(1)} fusion(f32[4,16,128,128]{3,2,1,0:T(8,128)} %copy-done.1, f32[4,15,128,128]{3,2,1,0:T(8,128)S(1)} %slice-done, f32[4,1,128,128]{3,2,1,0:T(8,128)S(1)} %broadcast_in_dim.81), kind=kOutput, calls=%fused_computation.4 | convolution fusion | flops 1611661312 | bytes 12582912 | tf_op jit(solution)/shard_map/...ij,...jk->...ik/dot_general | solution.py:14
  87.8 9.2 %fusion.37 = f32[4,16,128,128]{2,3,0,1:T(8,128)S(1)} fusion(f32[4,16,128,128]{2,3,0,1:T(8,128)S(1)} %copy-done.8, f32[4,14,128,128]{2,3,0,1:T(8,128)S(1)} %slice-done.4, f32[4,16,128,128]{3,2,1,0:T(8,128)S(1)} %fusion.3), kind=kOutput, calls=%fused_computation.39 | convolution fusion | flops 1611661312 | bytes 16252928 | tf_op jit(solution)/shard_map/...ij,...jk->...ik/dot_general | solution.py:14
  100.6 6.8 %fusion.7 = f32[4,16,128,128]{3,2,1,0:T(8,128)S(1)} fusion(f32[4,16,128,128]{3,2,1,0:T(8,128)} %copy-done.2, f32[4,14,128,128]{3,2,1,0:T(8,128)S(1)} %slice-done.1, f32[4,2,128,128]{3,2,1,0:T(8,128)S(1)} %slice.87), kind=kOutput, calls=%fused_computation.8 | convolution fusion | flops 1611661312 | bytes 12582912 | tf_op jit(solution)/shard_map/...ij,...jk->...ik/dot_general | solution.py:14
  110.9 9.2 %fusion.42 = f32[4,16,128,128]{2,3,0,1:T(8,128)S(1)} fusion(f32[4,16,128,128]{2,3,0,1:T(8,128)S(1)} %copy-done.10, f32[4,12,128,128]{2,3,0,1:T(8,128)S(1)} %slice-done.5, f32[4,16,128,128]{3,2,1,0:T(8,128)S(1)} %fusion.7), kind=kOutput, calls=%fused_computation.40 | convolution fusion | flops 1611661312 | bytes 15728640 | tf_op jit(solution)/shard_map/...ij,...jk->...ik/dot_general | solution.py:14
  123.5 6.4 %fusion.11 = f32[4,16,128,128]{3,2,1,0:T(8,128)S(1)} fusion(f32[4,16,128,128]{3,2,1,0:T(8,128)} %copy-done.3, f32[4,12,128,128]{3,2,1,0:T(8,128)S(1)} %slice-done.2, f32[4,4,128,128]{3,2,1,0:T(8,128)S(1)} %slice.89), kind=kOutput, calls=%fused_computation.12 | convolution fusion | flops 1611661312 | bytes 12582912 | tf_op jit(solution)/shard_map/...ij,...jk->...ik/dot_general | solution.py:14
  133.0 8.8 %fusion.47 = f32[4,16,128,128]{2,3,0,1:T(8,128)S(1)} fusion(f32[4,16,128,128]{2,3,0,1:T(8,128)S(1)} %copy-done.12, f32[4,8,128,128]{2,3,0,1:T(8,128)S(1)} %slice-done.6, f32[4,16,128,128]{3,2,1,0:T(8,128)S(1)} %fusion.11), kind=kOutput, calls=%fused_computation.41 | convolution fusion | flops 1611661312 | bytes 14680064 | tf_op jit(solution)/shard_map/...ij,...jk->...ik/dot_general | solution.py:14
  142.1 2.8 %slice-done.3 = f32[4,8,128,128]{3,2,1,0:T(8,128)S(1)} async-done(((f32[4,16,128,128]{3,2,1,0:T(8,128)}), f32[4,8,128,128]{3,2,1,0:T(8,128)S(1)}, s32[]{:S(2)}) %slice-start.3) | async-done | bytes 2097176 | tf_op jit(solution)/shard_map/slice | solution.py:79
  145.0 8.8 %fusion.15 = f32[4,16,128,128]{2,3,1,0:T(8,128)S(1)} fusion(f32[4,16,128,128]{3,2,1,0:T(8,128)} %copy-done.4, f32[4,8,128,128]{3,2,1,0:T(8,128)S(1)} %slice-done.3, f32[4,8,128,128]{3,2,1,0:T(8,128)S(1)} %slice.91), kind=kOutput, calls=%fused_computation.16 | convolution fusion | flops 1611661312 | bytes 12582912 | tf_op jit(solution)/shard_map/...ij,...jk->...ik/dot_general | solution.py:14
  160.7 3.4 %convolution_select_fusion = f32[4,16,32,64]{3,2,1,0:T(8,128)S(1)} fusion(f32[4,16,64,128]{3,2,1,0:T(8,128)S(1)} %bitcast_multiply_fusion, f32[16,32,4,128]{3,2,1,0:T(4,128)S(1)} %reshape.56, f32[4,16,32]{2,1,0:T(8,128)S(1)} %add_rsqrt_fusion.1, pred[32,64]{1,0:T(8,128)(4,1)S(1)} %iota_compare_fusion.3), kind=kOutput, calls=%fused_computation.75 | convolution fusion | flops 201719808 | bytes 3680256 | tf_op jit(solution)/shard_map/...id,...jd->...ij/dot_general | solution.py:14
  171.3 3.8 %collective-permute-start.1 = (f32[4,128,256]{1,2,0:T(8,128)}, f32[4,128,256]{1,2,0:T(8,128)}, u32[]{:S(2)}, u32[]{:S(2)}) collective-permute-start(f32[4,128,256]{1,2,0:T(8,128)} %pad_maximum_fusion.1), channel_id=1, source_target_pairs={{0,8},{4,12},{8,16},{12,20},{16,24},{20,28},{24,32},{28,36},{32,40... | collective-permute-start | bytes 1572872 | tf_op jit(solution)/shard_map/ppermute | solution.py:98
  175.1 8.8 %fusion.23 = f32[4,16,32,128]{3,2,1,0:T(8,128)} fusion(f32[4,16,32,128]{3,2,1,0:T(8,128)S(1)} %fusion.80, f32[4,16,128,128]{2,3,0,1:T(8,128)} %copy-done.16), kind=kOutput, calls=%fused_computation.24 | convolution fusion | flops 402653184 | bytes 6029312 | tf_op jit(solution)/shard_map/hbcd,hbde->hbce/dot_general | solution.py:14
  185.1 4.0 %fusion.83 = f32[4,16,32,128]{3,2,1,0:T(8,128)S(1)} fusion(f32[4,16,32,128]{3,2,1,0:T(8,128)} %fusion.23, f32[4,16,32,64]{3,2,1,0:T(8,128)S(1)} %copy-done.18, f32[4,16,64,256]{3,2,1,0:T(8,128)} %copy-done.5), kind=kOutput, calls=%fused_computation.77 | convolution fusion | flops 201588736 | bytes 4718592 | tf_op jit(solution)/shard_map/...ij,...jd->...id/dot_general | solution.py:14
  192.8 5.4 %collective-permute-start.2 = (f32[4,128,256]{1,2,0:T(8,128)}, f32[4,128,256]{1,2,0:T(8,128)}, u32[]{:S(2)}, u32[]{:S(2)}) collective-permute-start(f32[4,128,256]{1,2,0:T(8,128)} %pad_maximum_fusion.2), channel_id=1, source_target_pairs={{0,16},{4,20},{8,24},{12,28},{16,32},{20,36},{24,40},{28,44},{32,4... | collective-permute-start | bytes 1572872 | tf_op jit(solution)/shard_map/ppermute | solution.py:98
  198.2 7.7 %fusion.19 = f32[4,16,32,128]{3,2,1,0:T(8,128)} fusion(f32[4,16,32,128]{3,2,1,0:T(8,128)S(1)} %fusion.80, f32[4,15,128,128]{2,3,1,0:T(8,128)S(1)} %slice-done.7, f32[4,1,128,128]{2,3,1,0:T(8,128)S(1)} %broadcast_in_dim.81.clone), kind=kOutput, calls=%fused_computation.20 | convolution fusion | flops 403701760 | bytes 6291456 | tf_op jit(solution)/shard_map/hbcd,hbde->hbce/dot_general | solution.py:14
  208.9 3.3 %collective-permute-done.2 = f32[4,128,256]{1,2,0:T(8,128)} collective-permute-done((f32[4,128,256]{1,2,0:T(8,128)}, f32[4,128,256]{1,2,0:T(8,128)}, u32[]{:S(2)}, u32[]{:S(2)}) %collective-permute-start.2) | collective-permute-done | bytes 524320 | tf_op jit(solution)/shard_map/ppermute | solution.py:98
  215.0 3.2 %collective-permute-start.3 = (f32[4,128,256]{1,2,0:T(8,128)S(1)}, f32[4,128,256]{1,2,0:T(8,128)S(1)}, u32[]{:S(2)}, u32[]{:S(2)}) collective-permute-start(f32[4,128,256]{1,2,0:T(8,128)S(1)} %pad_maximum_fusion.3), channel_id=1, source_target_pairs={{0,32},{4,36},{8,40},{12,44},{16,48},{20,52},{24,56},{28,60},{32,6... | collective-permute-start | bytes 1572872 | tf_op jit(solution)/shard_map/ppermute | solution.py:98
  222.2 8.2 %collective-permute-done.3 = f32[4,128,256]{1,2,0:T(8,128)S(1)} collective-permute-done((f32[4,128,256]{1,2,0:T(8,128)S(1)}, f32[4,128,256]{1,2,0:T(8,128)S(1)}, u32[]{:S(2)}, u32[]{:S(2)}) %collective-permute-start.3) | collective-permute-done | bytes 524320 | tf_op jit(solution)/shard_map/ppermute | solution.py:98
  234.7 12.7 %collective-permute-done.4 = f32[4,128,256]{1,2,0:T(8,128)S(1)} collective-permute-done((f32[4,128,256]{1,2,0:T(8,128)S(1)}, f32[4,128,256]{1,2,0:T(8,128)S(1)}, u32[]{:S(2)}, u32[]{:S(2)}) %collective-permute-start.4) | collective-permute-done | bytes 524320 | tf_op jit(solution)/shard_map/ppermute | solution.py:98
  249.8 3.0 %collective-permute-start.7 = (bf16[512,512]{0,1:T(8,128)(2,1)S(1)}, bf16[512,512]{0,1:T(8,128)(2,1)S(1)}, u32[]{:S(2)}, u32[]{:S(2)}) collective-permute-start(bf16[512,512]{0,1:T(8,128)(2,1)S(1)} %bitcast.84), channel_id=1, source_target_pairs={{0,3},{1,0},{2,1},{3,2},{4,7},{5,4},{6,5},{7,6},{8,11},{9,8},{10,9... | collective-permute-start | bytes 1572872 | tf_op jit(solution)/shard_map/ppermute | solution.py:156
  256.8 16.7 %collective-permute-done.7 = bf16[512,512]{0,1:T(8,128)(2,1)S(1)} collective-permute-done((bf16[512,512]{0,1:T(8,128)(2,1)S(1)}, bf16[512,512]{0,1:T(8,128)(2,1)S(1)}, u32[]{:S(2)}, u32[]{:S(2)}) %collective-permute-start.7) | collective-permute-done | bytes 524320 | tf_op jit(solution)/shard_map/ppermute | solution.py:156
  278.6 2.5 fusion.87
  (164 shorter events, 92.3 us)
Async XLA Ops:
  0.0 247.8 %copy-start = (f32[4,128,128]{2,1,0:T(8,128)S(1)}, f32[4,128,128]{2,1,0:T(8,128)}, u32[]{:S(2)}) copy-start(f32[4,128,128]{2,1,0:T(8,128)} %param.8) | copy-start | bytes 786436
  12.4 3.5 %copy-start.29 = (s32[64]{0:T(128)S(1)}, s32[64]{0:T(128)}, u32[]{:S(2)}) copy-start(s32[64]{0:T(128)} %get-tuple-element.21) | copy-start | bytes 772
  12.4 3.5 %copy-start.30 = (s32[64]{0:T(128)S(1)}, s32[64]{0:T(128)}, u32[]{:S(2)}) copy-start(s32[64]{0:T(128)} %get-tuple-element.22) | copy-start | bytes 772
  12.4 3.5 %copy-start.31 = (s32[64]{0:T(128)S(1)}, s32[64]{0:T(128)}, u32[]{:S(2)}) copy-start(s32[64]{0:T(128)} %get-tuple-element.27) | copy-start | bytes 772
  12.4 3.5 %copy-start.32 = (s32[64]{0:T(128)S(1)}, s32[64]{0:T(128)}, u32[]{:S(2)}) copy-start(s32[64]{0:T(128)} %get-tuple-element.28) | copy-start | bytes 772
  12.4 3.5 %copy-start.33 = (pred[64]{0:T(512)(128)(4,1)S(1)}, pred[64]{0:T(512)(128)(4,1)}, u32[]{:S(2)}) copy-start(pred[64]{0:T(512)(128)(4,1)} %get-tuple-element.15) | copy-start | bytes 196
  48.2 7.4 %copy-start.5 = (f32[4,16,64,256]{3,2,1,0:T(8,128)}, f32[4,16,64,256]{3,2,1,0:T(8,128)S(1)}, u32[]{:S(2)}) copy-start(f32[4,16,64,256]{3,2,1,0:T(8,128)S(1)} %fusion) | copy-start | bytes 12582916
  73.8 3.6 %slice-start = ((f32[4,16,128,128]{3,2,1,0:T(8,128)}), f32[4,15,128,128]{3,2,1,0:T(8,128)S(1)}, s32[]{:S(2)}) async-start(f32[4,16,128,128]{3,2,1,0:T(8,128)} %copy-done.1), calls=%async_computation | async-start | bytes 7864320 | tf_op jit(solution)/shard_map/slice | solution.py:79
  77.5 8.9 %copy-start.8 = (f32[4,16,128,128]{2,3,0,1:T(8,128)S(1)}, f32[4,16,128,128]{2,3,0,1:T(8,128)}, u32[]{:S(2)}) copy-start(f32[4,16,128,128]{2,3,0,1:T(8,128)} %copy-done.7) | copy-start | bytes 12582916
  84.3 3.6 %slice-start.4 = ((f32[4,16,128,128]{2,3,0,1:T(8,128)}), f32[4,14,128,128]{2,3,0,1:T(8,128)S(1)}, s32[]{:S(2)}) async-start(f32[4,16,128,128]{2,3,0,1:T(8,128)} %copy-done.7), calls=%async_computation.4 | async-start | bytes 7340032 | tf_op jit(solution)/shard_map/slice | solution.py:80
  97.1 3.6 %slice-start.1 = ((f32[4,16,128,128]{3,2,1,0:T(8,128)}), f32[4,14,128,128]{3,2,1,0:T(8,128)S(1)}, s32[]{:S(2)}) async-start(f32[4,16,128,128]{3,2,1,0:T(8,128)} %copy-done.2), calls=%async_computation.1 | async-start | bytes 7340032 | tf_op jit(solution)/shard_map/slice | solution.py:79
  100.6 9.0 %copy-start.10 = (f32[4,16,128,128]{2,3,0,1:T(8,128)S(1)}, f32[4,16,128,128]{2,3,0,1:T(8,128)}, u32[]{:S(2)}) copy-start(f32[4,16,128,128]{2,3,0,1:T(8,128)} %copy-done.9) | copy-start | bytes 12582916
  123.5 8.6 %copy-start.12 = (f32[4,16,128,128]{2,3,0,1:T(8,128)S(1)}, f32[4,16,128,128]{2,3,0,1:T(8,128)}, u32[]{:S(2)}) copy-start(f32[4,16,128,128]{2,3,0,1:T(8,128)} %copy-done.11) | copy-start | bytes 12582916
  141.9 12.0 %copy-start.16 = (f32[4,16,128,128]{2,3,0,1:T(8,128)}, f32[4,16,128,128]{2,3,0,1:T(8,128)S(1)}, u32[]{:S(2)}) copy-start(f32[4,16,128,128]{2,3,0,1:T(8,128)S(1)} %fusion.47) | copy-start | bytes 12582916
  156.7 10.8 %collective-permute-start = (f32[4,128,256]{1,2,0:T(8,128)}, f32[4,128,256]{1,2,0:T(8,128)}, u32[]{:S(2)}, u32[]{:S(2)}) collective-permute-start(f32[4,128,256]{1,2,0:T(8,128)} %pad_maximum_fusion), channel_id=1, source_target_pairs={{0,4},{4,8},{8,12},{12,16},{16,20},{20,24},{24,28},{28,32},{32,36}... | collective-permute-start | bytes 1572872 | tf_op jit(solution)/shard_map/ppermute | solution.py:98
  168.9 6.2 %copy-start.26 = (f32[4,128,128]{1,2,0:T(8,128)}, f32[4,128,128]{1,2,0:T(8,128)S(1)}, u32[]{:S(2)}) copy-start(f32[4,128,128]{1,2,0:T(8,128)S(1)} %fusion.97) | copy-start | bytes 786436
  170.4 4.7 %copy-start.22 = (f32[4,128,128]{1,2,0:T(8,128)}, f32[4,128,128]{1,2,0:T(8,128)S(1)}, u32[]{:S(2)}) copy-start(f32[4,128,128]{1,2,0:T(8,128)S(1)} %convolution_select_fusion.8) | copy-start | bytes 786436
  171.3 17.8 %collective-permute-start.1 = (f32[4,128,256]{1,2,0:T(8,128)}, f32[4,128,256]{1,2,0:T(8,128)}, u32[]{:S(2)}, u32[]{:S(2)}) collective-permute-start(f32[4,128,256]{1,2,0:T(8,128)} %pad_maximum_fusion.1), channel_id=1, source_target_pairs={{0,8},{4,12},{8,16},{12,20},{16,24},{20,28},{24,32},{28,36},{32,40... | collective-permute-start | bytes 1572872 | tf_op jit(solution)/shard_map/ppermute | solution.py:98
  185.1 4.0 %copy-start.23 = (f32[4,128,128]{1,2,0:T(8,128)S(1)}, f32[4,128,128]{1,2,0:T(8,128)}, u32[]{:S(2)}) copy-start(f32[4,128,128]{1,2,0:T(8,128)} %copy-done.22) | copy-start | bytes 786436
  185.1 4.0 %copy-start.27 = (f32[4,128,128]{1,2,0:T(8,128)S(1)}, f32[4,128,128]{1,2,0:T(8,128)}, u32[]{:S(2)}) copy-start(f32[4,128,128]{1,2,0:T(8,128)} %copy-done.26) | copy-start | bytes 786436
  185.1 13.1 %slice-start.7 = ((f32[4,16,128,128]{2,3,1,0:T(8,128)}), f32[4,15,128,128]{2,3,1,0:T(8,128)S(1)}, s32[]{:S(2)}) async-start(f32[4,16,128,128]{2,3,1,0:T(8,128)} %copy-done.13), calls=%async_computation.7 | async-start | bytes 7864320 | tf_op jit(solution)/shard_map/slice | solution.py:129
  190.4 15.5 %copy-start.24 = (f32[4,128,128]{1,2,0:T(8,128)}, f32[4,128,128]{1,2,0:T(8,128)S(1)}, u32[]{:S(2)}) copy-start(f32[4,128,128]{1,2,0:T(8,128)S(1)} %fusion.96) | copy-start | bytes 786436
  191.9 14.0 %copy-start.20 = (f32[4,128,128]{1,2,0:T(8,128)}, f32[4,128,128]{1,2,0:T(8,128)S(1)}, u32[]{:S(2)}) copy-start(f32[4,128,128]{1,2,0:T(8,128)S(1)} %convolution_select_fusion.6) | copy-start | bytes 786436
  192.8 19.5 %collective-permute-start.2 = (f32[4,128,256]{1,2,0:T(8,128)}, f32[4,128,256]{1,2,0:T(8,128)}, u32[]{:S(2)}, u32[]{:S(2)}) collective-permute-start(f32[4,128,256]{1,2,0:T(8,128)} %pad_maximum_fusion.2), channel_id=1, source_target_pairs={{0,16},{4,20},{8,24},{12,28},{16,32},{20,36},{24,40},{28,44},{32,4... | collective-permute-start | bytes 1572872 | tf_op jit(solution)/shard_map/ppermute | solution.py:98
  205.9 6.3 %copy-start.21 = (f32[4,128,128]{1,2,0:T(8,128)S(1)}, f32[4,128,128]{1,2,0:T(8,128)}, u32[]{:S(2)}) copy-start(f32[4,128,128]{1,2,0:T(8,128)} %copy-done.20) | copy-start | bytes 786436
  205.9 6.3 %copy-start.25 = (f32[4,128,128]{1,2,0:T(8,128)S(1)}, f32[4,128,128]{1,2,0:T(8,128)}, u32[]{:S(2)}) copy-start(f32[4,128,128]{1,2,0:T(8,128)} %copy-done.24) | copy-start | bytes 786436
  215.0 15.5 %collective-permute-start.3 = (f32[4,128,256]{1,2,0:T(8,128)S(1)}, f32[4,128,256]{1,2,0:T(8,128)S(1)}, u32[]{:S(2)}, u32[]{:S(2)}) collective-permute-start(f32[4,128,256]{1,2,0:T(8,128)S(1)} %pad_maximum_fusion.3), channel_id=1, source_target_pairs={{0,32},{4,36},{8,40},{12,44},{16,48},{20,52},{24,56},{28,60},{32,6... | collective-permute-start | bytes 1572872 | tf_op jit(solution)/shard_map/ppermute | solution.py:98
  231.3 16.1 %collective-permute-start.4 = (f32[4,128,256]{1,2,0:T(8,128)S(1)}, f32[4,128,256]{1,2,0:T(8,128)S(1)}, u32[]{:S(2)}, u32[]{:S(2)}) collective-permute-start(f32[4,128,256]{1,2,0:T(8,128)S(1)} %pad_maximum_fusion.4), channel_id=1, source_target_pairs={{0,64},{4,68},{8,72},{12,76},{16,80},{20,84},{24,88},{28,92},{32,9... | collective-permute-start | bytes 1572872 | tf_op jit(solution)/shard_map/ppermute | solution.py:98
  234.3 14.5 %copy-start.19 = (f32[4,16,32,128]{3,2,1,0:T(8,128)S(1)}, f32[4,16,32,128]{3,2,1,0:T(8,128)}, u32[]{:S(2)}) copy-start(f32[4,16,32,128]{3,2,1,0:T(8,128)} %fusion.19) | copy-start | bytes 3145732
  249.8 23.7 %collective-permute-start.7 = (bf16[512,512]{0,1:T(8,128)(2,1)S(1)}, bf16[512,512]{0,1:T(8,128)(2,1)S(1)}, u32[]{:S(2)}, u32[]{:S(2)}) collective-permute-start(bf16[512,512]{0,1:T(8,128)(2,1)S(1)} %bitcast.84), channel_id=1, source_target_pairs={{0,3},{1,0},{2,1},{3,2},{4,7},{5,4},{6,5},{7,6},{8,11},{9,8},{10,9... | collective-permute-start | bytes 1572872 | tf_op jit(solution)/shard_map/ppermute | solution.py:156
  252.8 24.0 %collective-permute-start.5 = (bf16[512,512]{0,1:T(8,128)(2,1)S(1)}, bf16[512,512]{0,1:T(8,128)(2,1)S(1)}, u32[]{:S(2)}, u32[]{:S(2)}) collective-permute-start(bf16[512,512]{0,1:T(8,128)(2,1)S(1)} %bitcast.85), channel_id=1, source_target_pairs={{0,1},{1,2},{2,3},{3,0},{4,5},{5,6},{6,7},{7,4},{8,9},{9,10},{10,1... | collective-permute-start | bytes 1572872 | tf_op jit(solution)/shard_map/ppermute | solution.py:156
  252.8 25.7 %collective-permute-start.6 = (bf16[512,512]{0,1:T(8,128)(2,1)S(1)}, bf16[512,512]{0,1:T(8,128)(2,1)S(1)}, u32[]{:S(2)}, u32[]{:S(2)}) collective-permute-start(bf16[512,512]{0,1:T(8,128)(2,1)S(1)} %bitcast.86), channel_id=1, source_target_pairs={{0,2},{1,3},{2,0},{3,1},{4,6},{5,7},{6,4},{7,5},{8,10},{9,11},{10,... | collective-permute-start | bytes 1572872 | tf_op jit(solution)/shard_map/ppermute | solution.py:156
  (20 other events, 49.1 us)

commit v3 on v1

--- a/solution.py
+++ b/solution.py
@@ -71,15 +71,13 @@
 
 def block_prefix(moving, carried):
     count = moving.shape[1]
-    identity = jnp.broadcast_to(jnp.eye(moving.shape[-1], dtype=jnp.float32), moving.shape)
-    zeros = jnp.zeros_like(carried)
     shift = 1
     while shift < count:
-        earlier = (
-            jnp.concatenate([identity[:, :shift], moving[:, :-shift]], axis=1),
-            jnp.concatenate([zeros[:, :shift], carried[:, :-shift]], axis=1),
+        new_move, new_carry = compose(
+            (moving[:, :-shift], carried[:, :-shift]), (moving[:, shift:], carried[:, shift:])
         )
-        moving, carried = compose(earlier, (moving, carried))
+        moving = jnp.concatenate([moving[:, :shift], new_move], axis=1)
+        carried = jnp.concatenate([carried[:, :shift], new_carry], axis=1)
         shift *= 2
     return moving, carried
 
@@ -97,7 +95,7 @@
         pairs = [(i, i + shift) for i in range(count - shift)]
         got = jax.tree.map(lambda a: lax.ppermute(a, axis, pairs), span)
         valid = place >= shift
-        new_before = compose(got, before)
+        new_before = got if shift == 1 else compose(got, before)
         before = jax.tree.map(lambda n, o: jnp.where(valid, n, o), new_before, before)
         if 2 * shift < count:
             new_span = compose(got, span)

time: 227 us -> 221 us (0.974)
  matrix products: 129 us -> 122 us
  waiting for transfers between devices: 35.5 us -> 30.2 us
  other arithmetic: 5.91 us -> 11.1 us
  starting transfers between devices: 34.7 us -> 37.6 us
    ppermute x10, waiting for transfers between devices: 25.1 us -> 12.1 us  [shard_prefix(): got = jax.tree.map(lambda a: lax.ppermute(a, axis, pairs), span)]
    ppermute x3, waiting for transfers between devices: 10.4 us -> 18.1 us  [local(): received = lax.ppermute(attended, 'head', pairs)]
    dot_general x49 -> x47, matrix products: 121 us -> 115 us  [product(): return jnp.einsum(pattern, left, right, precision=lax.Precision.HIGHEST)]
    concatenate x0 -> x5, other arithmetic: none -> 5.23 us  [the longest x3 3.09 us: block_prefix(): carried = jnp.concatenate([carried[:, :shift], new_carry], axis=1)]
    slice x9 -> x4, local copies, waits for them, and re-layouts: 3.26 us -> 0.11 us  [the longest x2 0.11 us: block_prefix(): moving = jnp.concatenate([moving[:, :shift], new_move], axis=1)]
    ppermute x10, starting transfers between devices: 29.6 us -> 32.3 us  [shard_prefix(): got = jax.tree.map(lambda a: lax.ppermute(a, axis, pairs), span)]
  transfers between devices with their start and end apart: 13 -> 13, of which waited for: 8 -> 6; matrix products, arithmetic and copies ran while one was open for 29% -> 33% of each run, Pallas kernels for 0% -> 0%
where the time goes in v3:
time: 221 us; the launch traced here: 218 us
  matrix products  122 us (55%)
  starting transfers between devices  37.6 us (17%)
  waiting for transfers between devices  30.2 us (14%)
  local copies, waits for them, and re-layouts  15.5 us (7%)
  other arithmetic  11.1 us (5%)
    dot_general x47, matrix products, product(): return jnp.einsum(pattern, left, right, precision=lax.Precision.HIGHEST)  115 us
    ppermute x10, starting transfers between devices, shard_prefix(): got = jax.tree.map(lambda a: lax.ppermute(a, axis, pairs), span)  32.3 us
    ppermute x3, waiting for transfers between devices, local(): received = lax.ppermute(attended, 'head', pairs)  18.1 us
    ppermute x10, waiting for transfers between devices, shard_prefix(): got = jax.tree.map(lambda a: lax.ppermute(a, axis, pairs), span)  12.1 us
    dot_general x4, matrix products, partial(): return jnp.dot(block, rows, preferred_element_type=jnp.float32)  7.62 us
    ppermute x3, starting transfers between devices, local(): received = lax.ppermute(attended, 'head', pairs)  5.29 us
  transfers between devices with their start and end apart: 13, of which 6 were waited for; matrix products, arithmetic and copies ran while one was open for 33% of the time, Pallas kernels for 0%

profile of v3, /device:TPU:16, one launch (start us, length us, event | category | flops | bytes accessed | tf_op | source)
XLA Modules:
  0.0 217.7 jit_solution(13148964951374081475)
XLA Ops:
  12.0 3.4 %convolution_multiply_fusion = f32[4,16,64,64]{3,2,1,0:T(8,128)S(1)} fusion(f32[4,16,64,128]{3,2,1,0:T(8,128)S(1)} %bitcast_multiply_fusion, f32[64,64]{1,0:T(8,128)S(1)} %select_multiply_fusion), kind=kOutput, calls=%fused_computation.75 | convolution fusion | flops 402915328 | bytes 3162112 | tf_op jit(solution)/shard_map/...id,...jd->...ij/dot_general | solution.py:14
  22.0 2.6 %convolution_subtract_fusion.4 = f32[4,16,64,64]{3,2,1,0:T(8,128)S(1)} fusion(f32[4,16,64,64]{3,2,1,0:T(8,128)S(1)} %fusion.40, f32[4,16,64,64]{3,2,1,0:T(8,128)S(1)} %fusion.92, f32[64,64]{1,0:T(8,128)S(1)} %fusion.155), kind=kOutput, calls=%fused_computation.72 | convolution fusion | flops 201850880 | bytes 3162112 | tf_op jit(solution)/shard_map/...ij,...jk->...ik/dot_general | solution.py:14
  26.9 2.4 %convolution_subtract_fusion.3 = f32[4,16,64,64]{3,2,1,0:T(8,128)S(1)} fusion(f32[4,16,64,64]{3,2,1,0:T(8,128)S(1)} %convolution_subtract_fusion.4, f32[4,16,64,64]{3,2,1,0:T(8,128)S(1)} %fusion.38), kind=kOutput, calls=%fused_computation.71 | convolution fusion | flops 201588736 | bytes 3145728 | tf_op jit(solution)/shard_map/...ij,...jk->...ik/dot_general | solution.py:14
  31.6 2.4 %convolution_subtract_fusion.2 = f32[4,16,64,64]{3,2,1,0:T(8,128)S(1)} fusion(f32[4,16,64,64]{3,2,1,0:T(8,128)S(1)} %convolution_subtract_fusion.3, f32[4,16,64,64]{3,2,1,0:T(8,128)S(1)} %fusion.36), kind=kOutput, calls=%fused_computation.70 | convolution fusion | flops 201588736 | bytes 3145728 | tf_op jit(solution)/shard_map/...ij,...jk->...ik/dot_general | solution.py:14
  36.3 2.8 %convolution_subtract_fusion.1 = f32[4,16,64,64]{3,2,1,0:T(8,128)S(1)} fusion(f32[4,16,64,64]{3,2,1,0:T(8,128)S(1)} %convolution_subtract_fusion.2, f32[4,16,64,64]{3,2,1,0:T(8,128)S(1)} %fusion.34), kind=kOutput, calls=%fused_computation.69 | convolution fusion | flops 201588736 | bytes 3145728 | tf_op jit(solution)/shard_map/...ij,...jk->...ik/dot_general | solution.py:14
  43.7 4.3 %fusion.6 = f32[4,16,64,256]{3,2,1,0:T(8,128)S(1)} fusion(f32[4,16,64,128]{3,2,1,0:T(8,128)S(1)} %bitcast.98, f32[4,16,64,128]{3,2,1,0:T(8,128)S(1)} %bitcast_multiply_fusion, f32[4,16,64,64]{3,2,1,0:T(8,128)S(1)} %convolution_subtract_fusion.1, f32[4,16,64,64]{3,2,1,0:T(8,128)S(1)} %fusion.173), kind=kOutput, calls=%fused_computation.11 | convolution fusion | flops 807665664 | bytes 10485760 | tf_op jit(solution)/shard_map/...ij,...jk->...ik/dot_general | solution.py:14
  48.0 7.0 %convolution_subtract_fusion = f32[4,16,128,128]{3,2,1,0:T(8,128)S(1)} fusion(f32[4,16,64,128]{3,2,1,0:T(8,128)S(1)} %bitcast_multiply_fusion, f32[128,128]{1,0:T(8,128)S(1)} %fusion.116, f32[4,16,64,256]{3,2,1,0:T(8,128)S(1)} %fusion.6), kind=kOutput, calls=%fused_computation.38 | convolution fusion | flops 806354944 | bytes 8454144 | tf_op jit(solution)/shard_map/...cd,...ce->...de/dot_general | solution.py:14
  55.0 4.1 %fusion.12 = f32[4,15,128,128]{3,2,1,0:T(8,128)S(1)} fusion(f32[4,16,128,128]{3,2,1,0:T(8,128)S(1)} %convolution_subtract_fusion), kind=kOutput, calls=%fused_computation.18 | convolution fusion | flops 1509949440 | bytes 12058624 | tf_op jit(solution)/shard_map/...ij,...jk->...ik/dot_general | solution.py:14
  59.1 4.3 %fusion.19 = f32[4,14,128,128]{3,2,1,0:T(8,128)S(1)} fusion(f32[4,15,128,128]{3,2,1,0:T(8,128)S(1)} %fusion.12, f32[4,1,128,128]{3,2,1,0:T(8,128)S(1)} %slice.115), kind=kOutput, calls=%fused_computation.29 | convolution fusion | flops 1410203648 | bytes 7864320 | tf_op jit(solution)/shard_map/...ij,...jk->...ik/dot_general | solution.py:14
  65.3 3.5 %fusion.24 = f32[4,12,128,128]{3,2,1,0:T(8,128)S(1)} fusion(f32[4,14,128,128]{3,2,1,0:T(8,128)S(1)} %fusion.19, f32[4,16,128,128]{3,2,1,0:T(8,128)S(1)} %fusion.5), kind=kOutput, calls=%fused_computation.35 | convolution fusion | flops 1207959552 | bytes 9961472 | tf_op jit(solution)/shard_map/...ij,...jk->...ik/dot_general | solution.py:14
  74.2 6.8 %fusion.52 = f32[4,16,128,128]{3,2,1,0:T(8,128)S(1)} fusion(f32[4,16,64,128]{3,2,1,0:T(8,128)S(1)} %bitcast_multiply_fusion, f32[4,16,64,256]{3,2,1,0:T(8,128)S(1)} %fusion.6), kind=kOutput, calls=%fused_computation.64 | convolution fusion | flops 805306368 | bytes 8388608 | tf_op jit(solution)/shard_map/...cd,...ce->...de/dot_general | solution.py:14
  82.0 5.2 %copy_add_fusion = f32[4,15,128,128]{3,2,0,1:T(8,128)S(1)} fusion(f32[4,15,128,128]{3,2,1,0:T(8,128)S(1)} %get-tuple-element.6, f32[4,15,128,128]{3,2,1,0:T(8,128)S(1)} %get-tuple-element.5, f32[4,16,128,128]{3,2,1,0:T(8,128)S(1)} %convolution_subtract_fusion), kind=kOutput, calls=%fused_computation.20 | convolution fusion | flops 1510932480 | bytes 15728640 | tf_op jit(solution)/shard_map/...ij,...jk->...ik/dot_general | solution.py:14
  87.2 4.8 %slice_add_fusion = f32[4,14,128,128]{3,2,0,1:T(8,128)S(1)} fusion(f32[4,15,128,128]{3,2,0,1:T(8,128)S(1)} %copy_add_fusion, f32[4,1,128,128]{3,2,0,1:T(8,128)S(1)} %slice_bitcast_fusion.1, f32[4,15,128,128]{3,2,1,0:T(8,128)S(1)} %fusion.12), kind=kOutput, calls=%fused_computation.24 | convolution fusion | flops 1411121152 | bytes 15204352 | tf_op jit(solution)/shard_map/...ij,...jk->...ik/dot_general | solution.py:14
  94.1 3.9 %slice_add_fusion.1 = f32[4,12,128,128]{3,2,0,1:T(8,128)S(1)} fusion(f32[4,14,128,128]{3,2,0,1:T(8,128)S(1)} %slice_add_fusion, f32[4,16,128,128]{3,2,0,1:T(8,128)S(1)} %fusion, f32[4,14,128,128]{3,2,1,0:T(8,128)S(1)} %copy-done.7), kind=kOutput, calls=%fused_computation.32 | convolution fusion | flops 1208745984 | bytes 12582912 | tf_op jit(solution)/shard_map/...ij,...jk->...ik/dot_general | solution.py:14
  103.3 4.1 %collective-permute-start.5 = (f32[4,128,128]{2,1,0:T(8,128)}, f32[4,128,128]{2,1,0:T(8,128)}, u32[]{:S(2)}, u32[]{:S(2)}) collective-permute-start(f32[4,128,128]{2,1,0:T(8,128)} %slice_bitcast_fusion), channel_id=1, source_target_pairs={{0,4},{4,8},{8,12},{12,16},{16,20},{20,24},{24,28},{28,32},{32,36}... | collective-permute-start | bytes 786440 | tf_op jit(solution)/shard_map/ppermute | solution.py:96
  111.7 3.4 %convolution_select_fusion = f32[4,16,32,64]{3,2,1,0:T(8,128)S(1)} fusion(f32[4,16,64,128]{3,2,1,0:T(8,128)S(1)} %bitcast_multiply_fusion, f32[16,32,4,128]{3,2,1,0:T(4,128)S(1)} %reshape.56, f32[4,16,32]{2,1,0:T(8,128)S(1)} %add_rsqrt_fusion.1, pred[32,64]{1,0:T(8,128)(4,1)S(1)} %iota_compare_fusion.5), kind=kOutput, calls=%fused_computation.76 | convolution fusion | flops 201719808 | bytes 3680256 | tf_op jit(solution)/shard_map/...id,...jd->...ij/dot_general | solution.py:14
  117.2 3.7 %fusion.10 = f32[4,16,32,128]{3,2,1,0:T(8,128)S(1)} fusion(f32[4,16,32,128]{3,2,1,0:T(8,128)S(1)} %fusion.65, f32[4,15,128,128]{3,2,0,1:T(8,128)S(1)} %copy-done.5), kind=kOutput, calls=%fused_computation.15 | convolution fusion | flops 402653184 | bytes 6029312 | tf_op jit(solution)/shard_map/hbcd,hbde->hbce/dot_general | solution.py:14
  120.9 3.0 %fusion.68 = f32[4,16,32,128]{3,2,1,0:T(8,128)} fusion(f32[4,16,32,128]{3,2,1,0:T(8,128)S(1)} %fusion.10, f32[4,16,32,64]{3,2,1,0:T(8,128)S(1)} %convolution_select_fusion, f32[4,16,64,256]{3,2,1,0:T(8,128)S(1)} %copy-done.2), kind=kOutput, calls=%fused_computation.78 | convolution fusion | flops 201588736 | bytes 5242880 | tf_op jit(solution)/shard_map/...ij,...jd->...id/dot_general | solution.py:14
  124.0 2.8 %convolution_select_fusion.8 = f32[4,128,128]{2,1,0:T(8,128)} fusion(f32[4,128,128]{2,1,0:T(8,128)} %collective-permute-done, pred[]{:T(512)S(6)} %ge.28, f32[4,8,128,128]{3,2,1,0:T(8,128)} %copy-done.13), kind=kOutput, calls=%fused_computation.92 | convolution fusion | flops 100728832 | bytes 1048577 | tf_op jit(solution)/shard_map/...ij,...jk->...ik/dot_general | solution.py:14
  126.7 3.8 %collective-permute-start.1 = (f32[4,128,128]{2,1,0:T(8,128)}, f32[4,128,128]{2,1,0:T(8,128)}, u32[]{:S(2)}, u32[]{:S(2)}) collective-permute-start(f32[4,128,128]{2,1,0:T(8,128)} %convolution_select_fusion.8), channel_id=1, source_target_pairs={{0,8},{4,12},{8,16},{12,20},{16,24},{20,28},{24,32},{28,36},{32,40... | collective-permute-start | bytes 786440 | tf_op jit(solution)/shard_map/ppermute | solution.py:96
  132.8 3.5 %collective-permute-start.6 = (f32[4,128,128]{2,1,0:T(8,128)}, f32[4,128,128]{2,1,0:T(8,128)}, u32[]{:S(2)}, u32[]{:S(2)}) collective-permute-start(f32[4,128,128]{2,1,0:T(8,128)} %fusion.82), channel_id=1, source_target_pairs={{0,8},{4,12},{8,16},{12,20},{16,24},{20,28},{24,32},{28,36},{32,40... | collective-permute-start | bytes 786440 | tf_op jit(solution)/shard_map/ppermute | solution.py:96
  136.3 6.2 %fusion.2 = f32[4,16,32,128]{3,2,1,0:T(8,128)} fusion(f32[4,16,32,128]{3,2,1,0:T(8,128)S(1)} %fusion.65, f32[4,8,128,128]{3,2,1,0:T(8,128)} %copy-done.13, f32[4,8,128,128]{3,2,1,0:T(8,128)S(1)} %copy-done.11, f32[4,1,128,128]{3,2,1,0:T(8,128)S(1)} %broadcast_in_dim.75), kind=kOutput, calls=%fused_computation.5 | convolution fusion | flops 404750336 | bytes 6553600 | tf_op jit(solution)/shard_map/hbcd,hbde->hbce/dot_general | solution.py:14
  145.6 3.8 %collective-permute-start.2 = (f32[4,128,128]{2,1,0:T(8,128)S(1)}, f32[4,128,128]{2,1,0:T(8,128)S(1)}, u32[]{:S(2)}, u32[]{:S(2)}) collective-permute-start(f32[4,128,128]{2,1,0:T(8,128)S(1)} %convolution_select_fusion.6), channel_id=1, source_target_pairs={{0,16},{4,20},{8,24},{12,28},{16,32},{20,36},{24,40},{28,44},{32,4... | collective-permute-start | bytes 786440 | tf_op jit(solution)/shard_map/ppermute | solution.py:96
  150.9 4.3 %collective-permute-start.7 = (f32[4,128,128]{2,1,0:T(8,128)S(1)}, f32[4,128,128]{2,1,0:T(8,128)S(1)}, u32[]{:S(2)}, u32[]{:S(2)}) collective-permute-start(f32[4,128,128]{2,1,0:T(8,128)S(1)} %fusion.81), channel_id=1, source_target_pairs={{0,16},{4,20},{8,24},{12,28},{16,32},{20,36},{24,40},{28,44},{32,4... | collective-permute-start | bytes 786440 | tf_op jit(solution)/shard_map/ppermute | solution.py:96
  158.7 4.0 %collective-permute-start.3 = (f32[4,128,128]{2,1,0:T(8,128)S(1)}, f32[4,128,128]{2,1,0:T(8,128)S(1)}, u32[]{:S(2)}, u32[]{:S(2)}) collective-permute-start(f32[4,128,128]{2,1,0:T(8,128)S(1)} %convolution_select_fusion.4), channel_id=1, source_target_pairs={{0,32},{4,36},{8,40},{12,44},{16,48},{20,52},{24,56},{28,60},{32,6... | collective-permute-start | bytes 786440 | tf_op jit(solution)/shard_map/ppermute | solution.py:96
  164.4 3.9 %collective-permute-start.8 = (f32[4,128,128]{2,1,0:T(8,128)S(1)}, f32[4,128,128]{2,1,0:T(8,128)S(1)}, u32[]{:S(2)}, u32[]{:S(2)}) collective-permute-start(f32[4,128,128]{2,1,0:T(8,128)S(1)} %fusion.80), channel_id=1, source_target_pairs={{0,32},{4,36},{8,40},{12,44},{16,48},{20,52},{24,56},{28,60},{32,6... | collective-permute-start | bytes 786440 | tf_op jit(solution)/shard_map/ppermute | solution.py:96
  170.8 3.4 %collective-permute-done.8 = f32[4,128,128]{2,1,0:T(8,128)S(1)} collective-permute-done((f32[4,128,128]{2,1,0:T(8,128)S(1)}, f32[4,128,128]{2,1,0:T(8,128)S(1)}, u32[]{:S(2)}, u32[]{:S(2)}) %collective-permute-start.8) | collective-permute-done | bytes 262176 | tf_op jit(solution)/shard_map/ppermute | solution.py:96
  176.8 4.3 %collective-permute-done.4 = f32[4,128,128]{2,1,0:T(8,128)S(1)} collective-permute-done((f32[4,128,128]{2,1,0:T(8,128)S(1)}, f32[4,128,128]{2,1,0:T(8,128)S(1)}, u32[]{:S(2)}, u32[]{:S(2)}) %collective-permute-start.4) | collective-permute-done | bytes 262176 | tf_op jit(solution)/shard_map/ppermute | solution.py:96
  181.8 3.1 %collective-permute-done.9 = f32[4,128,128]{2,1,0:T(8,128)S(1)} collective-permute-done((f32[4,128,128]{2,1,0:T(8,128)S(1)}, f32[4,128,128]{2,1,0:T(8,128)S(1)}, u32[]{:S(2)}, u32[]{:S(2)}) %collective-permute-start.9) | collective-permute-done | bytes 262176 | tf_op jit(solution)/shard_map/ppermute | solution.py:96
  186.5 3.0 %collective-permute-start.12 = (bf16[512,512]{0,1:T(8,128)(2,1)S(1)}, bf16[512,512]{0,1:T(8,128)(2,1)S(1)}, u32[]{:S(2)}, u32[]{:S(2)}) collective-permute-start(bf16[512,512]{0,1:T(8,128)(2,1)S(1)} %bitcast.101), channel_id=1, source_target_pairs={{0,3},{1,0},{2,1},{3,2},{4,7},{5,4},{6,5},{7,6},{8,11},{9,8},{10,9... | collective-permute-start | bytes 1572872 | tf_op jit(solution)/shard_map/ppermute | solution.py:152
  193.5 16.4 %collective-permute-done.12 = bf16[512,512]{0,1:T(8,128)(2,1)S(1)} collective-permute-done((bf16[512,512]{0,1:T(8,128)(2,1)S(1)}, bf16[512,512]{0,1:T(8,128)(2,1)S(1)}, u32[]{:S(2)}, u32[]{:S(2)}) %collective-permute-start.12) | collective-permute-done | bytes 524320 | tf_op jit(solution)/shard_map/ppermute | solution.py:152
  215.0 2.5 %fusion.72 = bf16[512,512]{1,0:T(8,128)(2,1)} fusion(f32[512,512]{1,0:T(8,128)S(1)} %fusion.102, f32[512,512]{1,0:T(8,128)S(1)} %convolution_add_fusion.1, bf16[512,512]{0,1:T(8,128)(2,1)S(1)} %collective-permute-done.11, bf16[2048,2048]{1,0:T(8,128)(2,1)} %param.9, s32[]{:T(128)S(6)} %select_n.333, s32[]{:T(128)S(6)} %select_n.327), kind=kOutput, calls=%fused_computation.83 | convolution fusion | flops 269221888 | bytes 3670024 | tf_op jit(solution)/shard_map/dot_general | solution.py:147
  (129 shorter events, 79.7 us)
Async XLA Ops:
  0.0 181.4 %copy-start = (f32[4,128,128]{2,1,0:T(8,128)S(1)}, f32[4,128,128]{2,1,0:T(8,128)}, u32[]{:S(2)}) copy-start(f32[4,128,128]{2,1,0:T(8,128)} %param.8) | copy-start | bytes 786436
  5.7 2.2 %copy-start.14 = (bf16[512,2,512]{2,1,0:T(2,128)(2,1)S(1)}, bf16[512,2,512]{2,1,0:T(2,128)(2,1)}, u32[]{:S(2)}) copy-start(bf16[512,2,512]{2,1,0:T(2,128)(2,1)} %param.7) | copy-start | bytes 3145732
  12.0 3.5 %copy-start.15 = (s32[64]{0:T(128)S(1)}, s32[64]{0:T(128)}, u32[]{:S(2)}) copy-start(s32[64]{0:T(128)} %get-tuple-element.25) | copy-start | bytes 772
  12.0 3.5 %copy-start.16 = (s32[64]{0:T(128)S(1)}, s32[64]{0:T(128)}, u32[]{:S(2)}) copy-start(s32[64]{0:T(128)} %get-tuple-element.26) | copy-start | bytes 772
  12.0 3.5 %copy-start.17 = (s32[64]{0:T(128)S(1)}, s32[64]{0:T(128)}, u32[]{:S(2)}) copy-start(s32[64]{0:T(128)} %get-tuple-element.31) | copy-start | bytes 772
  12.0 3.5 %copy-start.18 = (s32[64]{0:T(128)S(1)}, s32[64]{0:T(128)}, u32[]{:S(2)}) copy-start(s32[64]{0:T(128)} %get-tuple-element.32) | copy-start | bytes 772
  12.0 3.5 %copy-start.19 = (pred[64]{0:T(512)(128)(4,1)S(1)}, pred[64]{0:T(512)(128)(4,1)}, u32[]{:S(2)}) copy-start(pred[64]{0:T(512)(128)(4,1)} %get-tuple-element.19) | copy-start | bytes 196
  12.0 3.5 %copy-start.20 = (pred[64]{0:T(512)(128)(4,1)S(1)}, pred[64]{0:T(512)(128)(4,1)}, u32[]{:S(2)}) copy-start(pred[64]{0:T(512)(128)(4,1)} %get-tuple-element.20) | copy-start | bytes 196
  48.0 26.1 %copy-start.1 = (f32[4,16,64,256]{3,2,1,0:T(8,128)}, f32[4,16,64,256]{3,2,1,0:T(8,128)S(1)}, u32[]{:S(2)}) copy-start(f32[4,16,64,256]{3,2,1,0:T(8,128)S(1)} %fusion.6) | copy-start | bytes 12582916
  68.7 2.3 %copy-start.9 = (f32[4,12,128,128]{3,2,1,0:T(8,128)}, f32[4,12,128,128]{3,2,1,0:T(8,128)S(1)}, u32[]{:S(2)}) copy-start(f32[4,12,128,128]{3,2,1,0:T(8,128)S(1)} %fusion.24) | copy-start | bytes 9437188
  71.0 3.1 %copy-start.13 = (f32[4,8,128,128]{3,2,1,0:T(8,128)}, f32[4,8,128,128]{3,2,1,0:T(8,128)S(1)}, u32[]{:S(2)}) copy-start(f32[4,8,128,128]{3,2,1,0:T(8,128)S(1)} %fusion.111) | copy-start | bytes 6291460
  71.8 52.1 %collective-permute-start = (f32[4,128,128]{2,1,0:T(8,128)}, f32[4,128,128]{2,1,0:T(8,128)}, u32[]{:S(2)}, u32[]{:S(2)}) collective-permute-start(f32[4,128,128]{2,1,0:T(8,128)} %slice_bitcast_fusion.2), channel_id=1, source_target_pairs={{0,4},{4,8},{8,12},{12,16},{16,20},{20,24},{24,28},{28,32},{32,36}... | collective-permute-start | bytes 786440 | tf_op jit(solution)/shard_map/ppermute | solution.py:96
  92.0 2.0 copy-start.7
  94.1 4.0 %copy-start.4 = (f32[4,16,128,128]{3,2,0,1:T(8,128)}, f32[4,16,128,128]{3,2,0,1:T(8,128)S(1)}, u32[]{:S(2)}) copy-start(f32[4,16,128,128]{3,2,0,1:T(8,128)S(1)} %fusion) | copy-start | bytes 12582916
  94.1 4.0 %copy-start.10 = (f32[4,12,128,128]{3,2,1,0:T(8,128)S(1)}, f32[4,12,128,128]{3,2,1,0:T(8,128)}, u32[]{:S(2)}) copy-start(f32[4,12,128,128]{3,2,1,0:T(8,128)} %copy-done.9) | copy-start | bytes 9437188
  102.5 4.9 %copy-start.8 = (f32[4,8,128,128]{3,2,0,1:T(8,128)}, f32[4,8,128,128]{3,2,0,1:T(8,128)S(1)}, u32[]{:S(2)}) copy-start(f32[4,8,128,128]{3,2,0,1:T(8,128)S(1)} %slice_add_fusion.2) | copy-start | bytes 6291460
  103.3 27.2 %collective-permute-start.5 = (f32[4,128,128]{2,1,0:T(8,128)}, f32[4,128,128]{2,1,0:T(8,128)}, u32[]{:S(2)}, u32[]{:S(2)}) collective-permute-start(f32[4,128,128]{2,1,0:T(8,128)} %slice_bitcast_fusion), channel_id=1, source_target_pairs={{0,4},{4,8},{8,12},{12,16},{16,20},{20,24},{24,28},{28,32},{32,36}... | collective-permute-start | bytes 786440 | tf_op jit(solution)/shard_map/ppermute | solution.py:96
  111.7 3.4 %copy-start.2 = (f32[4,16,64,256]{3,2,1,0:T(8,128)S(1)}, f32[4,16,64,256]{3,2,1,0:T(8,128)}, u32[]{:S(2)}) copy-start(f32[4,16,64,256]{3,2,1,0:T(8,128)} %copy-done.1) | copy-start | bytes 12582916
  115.1 2.1 copy-start.5
  123.9 12.4 %copy-start.11 = (f32[4,8,128,128]{3,2,1,0:T(8,128)S(1)}, f32[4,8,128,128]{3,2,1,0:T(8,128)}, u32[]{:S(2)}) copy-start(f32[4,8,128,128]{3,2,1,0:T(8,128)} %get-tuple-element.7) | copy-start | bytes 6291460
  126.7 17.4 %collective-permute-start.1 = (f32[4,128,128]{2,1,0:T(8,128)}, f32[4,128,128]{2,1,0:T(8,128)}, u32[]{:S(2)}, u32[]{:S(2)}) collective-permute-start(f32[4,128,128]{2,1,0:T(8,128)} %convolution_select_fusion.8), channel_id=1, source_target_pairs={{0,8},{4,12},{8,16},{12,20},{16,24},{20,28},{24,32},{28,36},{32,40... | collective-permute-start | bytes 786440 | tf_op jit(solution)/shard_map/ppermute | solution.py:96
  132.8 16.7 %collective-permute-start.6 = (f32[4,128,128]{2,1,0:T(8,128)}, f32[4,128,128]{2,1,0:T(8,128)}, u32[]{:S(2)}, u32[]{:S(2)}) collective-permute-start(f32[4,128,128]{2,1,0:T(8,128)} %fusion.82), channel_id=1, source_target_pairs={{0,8},{4,12},{8,16},{12,20},{16,24},{20,28},{24,32},{28,36},{32,40... | collective-permute-start | bytes 786440 | tf_op jit(solution)/shard_map/ppermute | solution.py:96
  145.6 12.6 %collective-permute-start.2 = (f32[4,128,128]{2,1,0:T(8,128)S(1)}, f32[4,128,128]{2,1,0:T(8,128)S(1)}, u32[]{:S(2)}, u32[]{:S(2)}) collective-permute-start(f32[4,128,128]{2,1,0:T(8,128)S(1)} %convolution_select_fusion.6), channel_id=1, source_target_pairs={{0,16},{4,20},{8,24},{12,28},{16,32},{20,36},{24,40},{28,44},{32,4... | collective-permute-start | bytes 786440 | tf_op jit(solution)/shard_map/ppermute | solution.py:96
  150.9 13.1 %collective-permute-start.7 = (f32[4,128,128]{2,1,0:T(8,128)S(1)}, f32[4,128,128]{2,1,0:T(8,128)S(1)}, u32[]{:S(2)}, u32[]{:S(2)}) collective-permute-start(f32[4,128,128]{2,1,0:T(8,128)S(1)} %fusion.81), channel_id=1, source_target_pairs={{0,16},{4,20},{8,24},{12,28},{16,32},{20,36},{24,40},{28,44},{32,4... | collective-permute-start | bytes 786440 | tf_op jit(solution)/shard_map/ppermute | solution.py:96
  158.7 10.5 %collective-permute-start.3 = (f32[4,128,128]{2,1,0:T(8,128)S(1)}, f32[4,128,128]{2,1,0:T(8,128)S(1)}, u32[]{:S(2)}, u32[]{:S(2)}) collective-permute-start(f32[4,128,128]{2,1,0:T(8,128)S(1)} %convolution_select_fusion.4), channel_id=1, source_target_pairs={{0,32},{4,36},{8,40},{12,44},{16,48},{20,52},{24,56},{28,60},{32,6... | collective-permute-start | bytes 786440 | tf_op jit(solution)/shard_map/ppermute | solution.py:96
  164.4 9.8 %collective-permute-start.8 = (f32[4,128,128]{2,1,0:T(8,128)S(1)}, f32[4,128,128]{2,1,0:T(8,128)S(1)}, u32[]{:S(2)}, u32[]{:S(2)}) collective-permute-start(f32[4,128,128]{2,1,0:T(8,128)S(1)} %fusion.80), channel_id=1, source_target_pairs={{0,32},{4,36},{8,40},{12,44},{16,48},{20,52},{24,56},{28,60},{32,6... | collective-permute-start | bytes 786440 | tf_op jit(solution)/shard_map/ppermute | solution.py:96
  169.5 11.5 %collective-permute-start.4 = (f32[4,128,128]{2,1,0:T(8,128)S(1)}, f32[4,128,128]{2,1,0:T(8,128)S(1)}, u32[]{:S(2)}, u32[]{:S(2)}) collective-permute-start(f32[4,128,128]{2,1,0:T(8,128)S(1)} %convolution_select_fusion.2), channel_id=1, source_target_pairs={{0,64},{4,68},{8,72},{12,76},{16,80},{20,84},{24,88},{28,92},{32,9... | collective-permute-start | bytes 786440 | tf_op jit(solution)/shard_map/ppermute | solution.py:96
  174.7 10.3 %collective-permute-start.9 = (f32[4,128,128]{2,1,0:T(8,128)S(1)}, f32[4,128,128]{2,1,0:T(8,128)S(1)}, u32[]{:S(2)}, u32[]{:S(2)}) collective-permute-start(f32[4,128,128]{2,1,0:T(8,128)S(1)} %fusion.79), channel_id=1, source_target_pairs={{0,64},{4,68},{8,72},{12,76},{16,80},{20,84},{24,88},{28,92},{32,9... | collective-permute-start | bytes 786440 | tf_op jit(solution)/shard_map/ppermute | solution.py:96
  176.4 9.0 %copy-start.12 = (f32[4,16,32,128]{3,2,1,0:T(8,128)S(1)}, f32[4,16,32,128]{3,2,1,0:T(8,128)}, u32[]{:S(2)}) copy-start(f32[4,16,32,128]{3,2,1,0:T(8,128)} %fusion.2) | copy-start | bytes 3145732
  186.5 23.4 %collective-permute-start.12 = (bf16[512,512]{0,1:T(8,128)(2,1)S(1)}, bf16[512,512]{0,1:T(8,128)(2,1)S(1)}, u32[]{:S(2)}, u32[]{:S(2)}) collective-permute-start(bf16[512,512]{0,1:T(8,128)(2,1)S(1)} %bitcast.101), channel_id=1, source_target_pairs={{0,3},{1,0},{2,1},{3,2},{4,7},{5,4},{6,5},{7,6},{8,11},{9,8},{10,9... | collective-permute-start | bytes 1572872 | tf_op jit(solution)/shard_map/ppermute | solution.py:152
  189.5 23.8 %collective-permute-start.10 = (bf16[512,512]{0,1:T(8,128)(2,1)S(1)}, bf16[512,512]{0,1:T(8,128)(2,1)S(1)}, u32[]{:S(2)}, u32[]{:S(2)}) collective-permute-start(bf16[512,512]{0,1:T(8,128)(2,1)S(1)} %bitcast.102), channel_id=1, source_target_pairs={{0,1},{1,2},{2,3},{3,0},{4,5},{5,6},{6,7},{7,4},{8,9},{9,10},{10,1... | collective-permute-start | bytes 1572872 | tf_op jit(solution)/shard_map/ppermute | solution.py:152
  189.5 25.5 %collective-permute-start.11 = (bf16[512,512]{0,1:T(8,128)(2,1)S(1)}, bf16[512,512]{0,1:T(8,128)(2,1)S(1)}, u32[]{:S(2)}, u32[]{:S(2)}) collective-permute-start(bf16[512,512]{0,1:T(8,128)(2,1)S(1)} %bitcast.103), channel_id=1, source_target_pairs={{0,2},{1,3},{2,0},{3,1},{4,6},{5,7},{6,4},{7,5},{8,10},{9,11},{10,... | collective-permute-start | bytes 1572872 | tf_op jit(solution)/shard_map/ppermute | solution.py:152
  (4 other events, 7.0 us)

commit v4 on v3

--- a/solution.py
+++ b/solution.py
@@ -29,9 +29,12 @@
             (rows // width) % 2 == 1
         ) & ((cols // width) % 2 == 0)
         coupling = jnp.where(lower_left, strict, 0.0)
-        inverse = inverse - product(
-            product(inverse, coupling, "...ij,...jk->...ik"), inverse, "...ij,...jk->...ik"
-        )
+        if width == 1:
+            inverse = inverse - coupling
+        else:
+            inverse = inverse - product(
+                product(inverse, coupling, "...ij,...jk->...ik"), inverse, "...ij,...jk->...ik"
+            )
         width *= 2
     return inverse
 

time: 221 us -> 217 us (0.982)
  matrix products: 122 us -> 119 us
    dot_general x47 -> x45, matrix products: 115 us -> 111 us  [product(): return jnp.einsum(pattern, left, right, precision=lax.Precision.HIGHEST)]
where the time goes in v4:
time: 217 us; the launch traced here: 214 us
  matrix products  119 us (55%)
  starting transfers between devices  37.3 us (17%)
  waiting for transfers between devices  30.2 us (14%)
  local copies, waits for them, and re-layouts  15.6 us (7%)
  other arithmetic  11.1 us (5%)
    dot_general x45, matrix products, product(): return jnp.einsum(pattern, left, right, precision=lax.Precision.HIGHEST)  111 us
    ppermute x10, starting transfers between devices, shard_prefix(): got = jax.tree.map(lambda a: lax.ppermute(a, axis, pairs), span)  31.9 us
    ppermute x3, waiting for transfers between devices, local(): received = lax.ppermute(attended, 'head', pairs)  18.1 us
    ppermute x10, waiting for transfers between devices, shard_prefix(): got = jax.tree.map(lambda a: lax.ppermute(a, axis, pairs), span)  12.1 us
    dot_general x4, matrix products, partial(): return jnp.dot(block, rows, preferred_element_type=jnp.float32)  7.62 us
    ppermute x3, starting transfers between devices, local(): received = lax.ppermute(attended, 'head', pairs)  5.37 us
  transfers between devices with their start and end apart: 13, of which 6 were waited for; matrix products, arithmetic and copies ran while one was open for 33% of the time, Pallas kernels for 0%

profile of v4, /device:TPU:16, one launch (start us, length us, event | category | flops | bytes accessed | tf_op | source)
XLA Modules:
  0.0 214.4 jit_solution(1691598996829142869)
XLA Ops:
  12.2 3.4 %convolution_multiply_fusion = f32[4,16,64,64]{3,2,1,0:T(8,128)S(1)} fusion(f32[4,16,64,128]{3,2,1,0:T(8,128)S(1)} %bitcast_multiply_fusion, f32[64,64]{1,0:T(8,128)S(1)} %select_multiply_fusion), kind=kOutput, calls=%fused_computation.73 | convolution fusion | flops 402915328 | bytes 3162112 | tf_op jit(solution)/shard_map/...id,...jd->...ij/dot_general | solution.py:14
  18.3 2.6 %fusion.42 = f32[4,16,64,64]{3,2,1,0:T(8,128)S(1)} fusion(f32[4,16,64,64]{3,2,1,0:T(8,128)S(1)} %convolution_multiply_fusion, f32[4,16,64,64]{3,2,1,0:T(8,128)S(1)} %fusion.40, f32[64,64]{1,0:T(8,128)S(1)} %fusion.151, pred[64,64]{1,0:T(8,128)(4,1)S(1)} %get-tuple-element.14), kind=kOutput, calls=%fused_computation.61 | convolution fusion | flops 202637312 | bytes 3166208 | tf_op jit(solution)/shard_map/...ij,...jk->...ik/dot_general | solution.py:14
  23.2 3.0 %convolution_subtract_fusion.3 = f32[4,16,64,64]{3,2,1,0:T(8,128)S(1)} fusion(f32[4,16,64,64]{3,2,1,0:T(8,128)S(1)} %fusion.42, f32[4,16,64,64]{3,2,1,0:T(8,128)S(1)} %fusion.38), kind=kOutput, calls=%fused_computation.72 | convolution fusion | flops 201588736 | bytes 3145728 | tf_op jit(solution)/shard_map/...ij,...jk->...ik/dot_general | solution.py:14
  28.5 2.4 %convolution_subtract_fusion.2 = f32[4,16,64,64]{3,2,1,0:T(8,128)S(1)} fusion(f32[4,16,64,64]{3,2,1,0:T(8,128)S(1)} %convolution_subtract_fusion.3, f32[4,16,64,64]{3,2,1,0:T(8,128)S(1)} %fusion.36), kind=kOutput, calls=%fused_computation.71 | convolution fusion | flops 201588736 | bytes 3145728 | tf_op jit(solution)/shard_map/...ij,...jk->...ik/dot_general | solution.py:14
  35.6 2.5 %fusion.32 = f32[4,16,64,64]{3,2,1,0:T(8,128)S(1)} fusion(f32[4,16,64,64]{3,2,1,0:T(8,128)S(1)} %convolution_subtract_fusion.1, f32[4,16,64,64]{3,2,1,0:T(8,128)S(1)} %convolution_multiply_fusion, pred[64,64]{1,0:T(8,128)(4,1)S(1)} %get-tuple-element.9), kind=kOutput, calls=%fused_computation.50 | convolution fusion | flops 201588736 | bytes 3149824 | tf_op jit(solution)/shard_map/...ij,...jk->...ik/dot_general | solution.py:14
  40.4 4.3 %fusion.6 = f32[4,16,64,256]{3,2,1,0:T(8,128)S(1)} fusion(f32[4,16,64,128]{3,2,1,0:T(8,128)S(1)} %bitcast.97, f32[4,16,64,128]{3,2,1,0:T(8,128)S(1)} %bitcast_multiply_fusion, f32[4,16,64,64]{3,2,1,0:T(8,128)S(1)} %convolution_subtract_fusion.1, f32[4,16,64,64]{3,2,1,0:T(8,128)S(1)} %fusion.169), kind=kOutput, calls=%fused_computation.11 | convolution fusion | flops 807665664 | bytes 10485760 | tf_op jit(solution)/shard_map/...ij,...jk->...ik/dot_general | solution.py:14
  44.7 7.2 %convolution_subtract_fusion = f32[4,16,128,128]{3,2,1,0:T(8,128)S(1)} fusion(f32[4,16,64,128]{3,2,1,0:T(8,128)S(1)} %bitcast_multiply_fusion, f32[128,128]{1,0:T(8,128)S(1)} %fusion.112, f32[4,16,64,256]{3,2,1,0:T(8,128)S(1)} %fusion.6), kind=kOutput, calls=%fused_computation.38 | convolution fusion | flops 806354944 | bytes 8454144 | tf_op jit(solution)/shard_map/...cd,...ce->...de/dot_general | solution.py:14
  52.0 4.1 %fusion.12 = f32[4,15,128,128]{3,2,1,0:T(8,128)S(1)} fusion(f32[4,16,128,128]{3,2,1,0:T(8,128)S(1)} %convolution_subtract_fusion), kind=kOutput, calls=%fused_computation.18 | convolution fusion | flops 1509949440 | bytes 12058624 | tf_op jit(solution)/shard_map/...ij,...jk->...ik/dot_general | solution.py:14
  56.1 4.1 %fusion.19 = f32[4,14,128,128]{3,2,1,0:T(8,128)S(1)} fusion(f32[4,15,128,128]{3,2,1,0:T(8,128)S(1)} %fusion.12, f32[4,1,128,128]{3,2,1,0:T(8,128)S(1)} %slice.115), kind=kOutput, calls=%fused_computation.29 | convolution fusion | flops 1410203648 | bytes 7864320 | tf_op jit(solution)/shard_map/...ij,...jk->...ik/dot_general | solution.py:14
  62.0 3.6 %fusion.24 = f32[4,12,128,128]{3,2,1,0:T(8,128)S(1)} fusion(f32[4,14,128,128]{3,2,1,0:T(8,128)S(1)} %fusion.19, f32[4,16,128,128]{3,2,1,0:T(8,128)S(1)} %fusion.5), kind=kOutput, calls=%fused_computation.35 | convolution fusion | flops 1207959552 | bytes 9961472 | tf_op jit(solution)/shard_map/...ij,...jk->...ik/dot_general | solution.py:14
  70.7 6.8 %fusion.52 = f32[4,16,128,128]{3,2,1,0:T(8,128)S(1)} fusion(f32[4,16,64,128]{3,2,1,0:T(8,128)S(1)} %bitcast_multiply_fusion, f32[4,16,64,256]{3,2,1,0:T(8,128)S(1)} %fusion.6), kind=kOutput, calls=%fused_computation.65 | convolution fusion | flops 805306368 | bytes 8388608 | tf_op jit(solution)/shard_map/...cd,...ce->...de/dot_general | solution.py:14
  78.5 5.5 %copy_add_fusion = f32[4,15,128,128]{3,2,0,1:T(8,128)S(1)} fusion(f32[4,15,128,128]{3,2,1,0:T(8,128)S(1)} %get-tuple-element.6, f32[4,15,128,128]{3,2,1,0:T(8,128)S(1)} %get-tuple-element.5, f32[4,16,128,128]{3,2,1,0:T(8,128)S(1)} %convolution_subtract_fusion), kind=kOutput, calls=%fused_computation.20 | convolution fusion | flops 1510932480 | bytes 15728640 | tf_op jit(solution)/shard_map/...ij,...jk->...ik/dot_general | solution.py:14
  84.0 4.8 %slice_add_fusion = f32[4,14,128,128]{3,2,0,1:T(8,128)S(1)} fusion(f32[4,15,128,128]{3,2,0,1:T(8,128)S(1)} %copy_add_fusion, f32[4,1,128,128]{3,2,0,1:T(8,128)S(1)} %slice_bitcast_fusion.1, f32[4,15,128,128]{3,2,1,0:T(8,128)S(1)} %fusion.12), kind=kOutput, calls=%fused_computation.24 | convolution fusion | flops 1411121152 | bytes 15204352 | tf_op jit(solution)/shard_map/...ij,...jk->...ik/dot_general | solution.py:14
  90.8 3.9 %slice_add_fusion.1 = f32[4,12,128,128]{3,2,0,1:T(8,128)S(1)} fusion(f32[4,14,128,128]{3,2,0,1:T(8,128)S(1)} %slice_add_fusion, f32[4,16,128,128]{3,2,0,1:T(8,128)S(1)} %fusion, f32[4,14,128,128]{3,2,1,0:T(8,128)S(1)} %copy-done.7), kind=kOutput, calls=%fused_computation.32 | convolution fusion | flops 1208745984 | bytes 12582912 | tf_op jit(solution)/shard_map/...ij,...jk->...ik/dot_general | solution.py:14
  100.0 4.1 %collective-permute-start.5 = (f32[4,128,128]{2,1,0:T(8,128)}, f32[4,128,128]{2,1,0:T(8,128)}, u32[]{:S(2)}, u32[]{:S(2)}) collective-permute-start(f32[4,128,128]{2,1,0:T(8,128)} %slice_bitcast_fusion), channel_id=1, source_target_pairs={{0,4},{4,8},{8,12},{12,16},{16,20},{20,24},{24,28},{28,32},{32,36}... | collective-permute-start | bytes 786440 | tf_op jit(solution)/shard_map/ppermute | solution.py:99
  108.4 3.4 %convolution_select_fusion = f32[4,16,32,64]{3,2,1,0:T(8,128)S(1)} fusion(f32[4,16,64,128]{3,2,1,0:T(8,128)S(1)} %bitcast_multiply_fusion, f32[16,32,4,128]{3,2,1,0:T(4,128)S(1)} %reshape.56, f32[4,16,32]{2,1,0:T(8,128)S(1)} %add_rsqrt_fusion.1, pred[32,64]{1,0:T(8,128)(4,1)S(1)} %iota_compare_fusion.5), kind=kOutput, calls=%fused_computation.74 | convolution fusion | flops 201719808 | bytes 3680256 | tf_op jit(solution)/shard_map/...id,...jd->...ij/dot_general | solution.py:14
  113.9 3.7 %fusion.10 = f32[4,16,32,128]{3,2,1,0:T(8,128)S(1)} fusion(f32[4,16,32,128]{3,2,1,0:T(8,128)S(1)} %fusion.63, f32[4,15,128,128]{3,2,0,1:T(8,128)S(1)} %copy-done.5), kind=kOutput, calls=%fused_computation.15 | convolution fusion | flops 402653184 | bytes 6029312 | tf_op jit(solution)/shard_map/hbcd,hbde->hbce/dot_general | solution.py:14
  117.6 3.0 %fusion.66 = f32[4,16,32,128]{3,2,1,0:T(8,128)} fusion(f32[4,16,32,128]{3,2,1,0:T(8,128)S(1)} %fusion.10, f32[4,16,32,64]{3,2,1,0:T(8,128)S(1)} %convolution_select_fusion, f32[4,16,64,256]{3,2,1,0:T(8,128)S(1)} %copy-done.2), kind=kOutput, calls=%fused_computation.76 | convolution fusion | flops 201588736 | bytes 5242880 | tf_op jit(solution)/shard_map/...ij,...jd->...id/dot_general | solution.py:14
  120.7 2.6 %convolution_select_fusion.8 = f32[4,128,128]{2,1,0:T(8,128)} fusion(f32[4,128,128]{2,1,0:T(8,128)} %collective-permute-done, pred[]{:T(512)S(6)} %ge.28, f32[4,8,128,128]{3,2,1,0:T(8,128)} %copy-done.13), kind=kOutput, calls=%fused_computation.90 | convolution fusion | flops 100728832 | bytes 1048577 | tf_op jit(solution)/shard_map/...ij,...jk->...ik/dot_general | solution.py:14
  123.2 3.8 %collective-permute-start.1 = (f32[4,128,128]{2,1,0:T(8,128)}, f32[4,128,128]{2,1,0:T(8,128)}, u32[]{:S(2)}, u32[]{:S(2)}) collective-permute-start(f32[4,128,128]{2,1,0:T(8,128)} %convolution_select_fusion.8), channel_id=1, source_target_pairs={{0,8},{4,12},{8,16},{12,20},{16,24},{20,28},{24,32},{28,36},{32,40... | collective-permute-start | bytes 786440 | tf_op jit(solution)/shard_map/ppermute | solution.py:99
  129.3 3.5 %collective-permute-start.6 = (f32[4,128,128]{2,1,0:T(8,128)}, f32[4,128,128]{2,1,0:T(8,128)}, u32[]{:S(2)}, u32[]{:S(2)}) collective-permute-start(f32[4,128,128]{2,1,0:T(8,128)} %fusion.80), channel_id=1, source_target_pairs={{0,8},{4,12},{8,16},{12,20},{16,24},{20,28},{24,32},{28,36},{32,40... | collective-permute-start | bytes 786440 | tf_op jit(solution)/shard_map/ppermute | solution.py:99
  132.8 6.2 %fusion.2 = f32[4,16,32,128]{3,2,1,0:T(8,128)} fusion(f32[4,16,32,128]{3,2,1,0:T(8,128)S(1)} %fusion.63, f32[4,8,128,128]{3,2,1,0:T(8,128)} %copy-done.13, f32[4,8,128,128]{3,2,1,0:T(8,128)S(1)} %copy-done.11, f32[4,1,128,128]{3,2,1,0:T(8,128)S(1)} %broadcast_in_dim.71), kind=kOutput, calls=%fused_computation.5 | convolution fusion | flops 404750336 | bytes 6553600 | tf_op jit(solution)/shard_map/hbcd,hbde->hbce/dot_general | solution.py:14
  142.2 3.8 %collective-permute-start.2 = (f32[4,128,128]{2,1,0:T(8,128)S(1)}, f32[4,128,128]{2,1,0:T(8,128)S(1)}, u32[]{:S(2)}, u32[]{:S(2)}) collective-permute-start(f32[4,128,128]{2,1,0:T(8,128)S(1)} %convolution_select_fusion.6), channel_id=1, source_target_pairs={{0,16},{4,20},{8,24},{12,28},{16,32},{20,36},{24,40},{28,44},{32,4... | collective-permute-start | bytes 786440 | tf_op jit(solution)/shard_map/ppermute | solution.py:99
  147.5 4.3 %collective-permute-start.7 = (f32[4,128,128]{2,1,0:T(8,128)S(1)}, f32[4,128,128]{2,1,0:T(8,128)S(1)}, u32[]{:S(2)}, u32[]{:S(2)}) collective-permute-start(f32[4,128,128]{2,1,0:T(8,128)S(1)} %fusion.79), channel_id=1, source_target_pairs={{0,16},{4,20},{8,24},{12,28},{16,32},{20,36},{24,40},{28,44},{32,4... | collective-permute-start | bytes 786440 | tf_op jit(solution)/shard_map/ppermute | solution.py:99
  155.2 4.0 %collective-permute-start.3 = (f32[4,128,128]{2,1,0:T(8,128)S(1)}, f32[4,128,128]{2,1,0:T(8,128)S(1)}, u32[]{:S(2)}, u32[]{:S(2)}) collective-permute-start(f32[4,128,128]{2,1,0:T(8,128)S(1)} %convolution_select_fusion.4), channel_id=1, source_target_pairs={{0,32},{4,36},{8,40},{12,44},{16,48},{20,52},{24,56},{28,60},{32,6... | collective-permute-start | bytes 786440 | tf_op jit(solution)/shard_map/ppermute | solution.py:99
  161.0 3.9 %collective-permute-start.8 = (f32[4,128,128]{2,1,0:T(8,128)S(1)}, f32[4,128,128]{2,1,0:T(8,128)S(1)}, u32[]{:S(2)}, u32[]{:S(2)}) collective-permute-start(f32[4,128,128]{2,1,0:T(8,128)S(1)} %fusion.78), channel_id=1, source_target_pairs={{0,32},{4,36},{8,40},{12,44},{16,48},{20,52},{24,56},{28,60},{32,6... | collective-permute-start | bytes 786440 | tf_op jit(solution)/shard_map/ppermute | solution.py:99
  167.4 3.4 %collective-permute-done.8 = f32[4,128,128]{2,1,0:T(8,128)S(1)} collective-permute-done((f32[4,128,128]{2,1,0:T(8,128)S(1)}, f32[4,128,128]{2,1,0:T(8,128)S(1)}, u32[]{:S(2)}, u32[]{:S(2)}) %collective-permute-start.8) | collective-permute-done | bytes 262176 | tf_op jit(solution)/shard_map/ppermute | solution.py:99
  173.3 4.3 %collective-permute-done.4 = f32[4,128,128]{2,1,0:T(8,128)S(1)} collective-permute-done((f32[4,128,128]{2,1,0:T(8,128)S(1)}, f32[4,128,128]{2,1,0:T(8,128)S(1)}, u32[]{:S(2)}, u32[]{:S(2)}) %collective-permute-start.4) | collective-permute-done | bytes 262176 | tf_op jit(solution)/shard_map/ppermute | solution.py:99
  178.4 3.1 %collective-permute-done.9 = f32[4,128,128]{2,1,0:T(8,128)S(1)} collective-permute-done((f32[4,128,128]{2,1,0:T(8,128)S(1)}, f32[4,128,128]{2,1,0:T(8,128)S(1)}, u32[]{:S(2)}, u32[]{:S(2)}) %collective-permute-start.9) | collective-permute-done | bytes 262176 | tf_op jit(solution)/shard_map/ppermute | solution.py:99
  183.0 3.1 %collective-permute-start.12 = (bf16[512,512]{0,1:T(8,128)(2,1)S(1)}, bf16[512,512]{0,1:T(8,128)(2,1)S(1)}, u32[]{:S(2)}, u32[]{:S(2)}) collective-permute-start(bf16[512,512]{0,1:T(8,128)(2,1)S(1)} %bitcast.100), channel_id=1, source_target_pairs={{0,3},{1,0},{2,1},{3,2},{4,7},{5,4},{6,5},{7,6},{8,11},{9,8},{10,9... | collective-permute-start | bytes 1572872 | tf_op jit(solution)/shard_map/ppermute | solution.py:155
  190.1 16.4 %collective-permute-done.12 = bf16[512,512]{0,1:T(8,128)(2,1)S(1)} collective-permute-done((bf16[512,512]{0,1:T(8,128)(2,1)S(1)}, bf16[512,512]{0,1:T(8,128)(2,1)S(1)}, u32[]{:S(2)}, u32[]{:S(2)}) %collective-permute-start.12) | collective-permute-done | bytes 524320 | tf_op jit(solution)/shard_map/ppermute | solution.py:155
  211.6 2.5 %fusion.70 = bf16[512,512]{1,0:T(8,128)(2,1)} fusion(f32[512,512]{1,0:T(8,128)S(1)} %fusion.98, f32[512,512]{1,0:T(8,128)S(1)} %convolution_add_fusion.1, bf16[512,512]{0,1:T(8,128)(2,1)S(1)} %collective-permute-done.11, bf16[2048,2048]{1,0:T(8,128)(2,1)} %param.9, s32[]{:T(128)S(6)} %select_n.333, s32[]{:T(128)S(6)} %select_n.327), kind=kOutput, calls=%fused_computation.81 | convolution fusion | flops 269221888 | bytes 3670024 | tf_op jit(solution)/shard_map/dot_general | solution.py:150
  (127 shorter events, 75.8 us)
Async XLA Ops:
  0.0 178.0 %copy-start = (f32[4,128,128]{2,1,0:T(8,128)S(1)}, f32[4,128,128]{2,1,0:T(8,128)}, u32[]{:S(2)}) copy-start(f32[4,128,128]{2,1,0:T(8,128)} %param.8) | copy-start | bytes 786436
  5.7 2.2 %copy-start.14 = (bf16[512,2,512]{2,1,0:T(2,128)(2,1)S(1)}, bf16[512,2,512]{2,1,0:T(2,128)(2,1)}, u32[]{:S(2)}) copy-start(bf16[512,2,512]{2,1,0:T(2,128)(2,1)} %param.7) | copy-start | bytes 3145732
  12.1 3.5 %copy-start.15 = (s32[64]{0:T(128)S(1)}, s32[64]{0:T(128)}, u32[]{:S(2)}) copy-start(s32[64]{0:T(128)} %get-tuple-element.25) | copy-start | bytes 772
  12.1 3.5 %copy-start.16 = (s32[64]{0:T(128)S(1)}, s32[64]{0:T(128)}, u32[]{:S(2)}) copy-start(s32[64]{0:T(128)} %get-tuple-element.26) | copy-start | bytes 772
  12.1 3.5 %copy-start.17 = (s32[64]{0:T(128)S(1)}, s32[64]{0:T(128)}, u32[]{:S(2)}) copy-start(s32[64]{0:T(128)} %get-tuple-element.31) | copy-start | bytes 772
  12.1 3.5 %copy-start.18 = (s32[64]{0:T(128)S(1)}, s32[64]{0:T(128)}, u32[]{:S(2)}) copy-start(s32[64]{0:T(128)} %get-tuple-element.32) | copy-start | bytes 772
  12.1 3.5 %copy-start.19 = (pred[64]{0:T(512)(128)(4,1)S(1)}, pred[64]{0:T(512)(128)(4,1)}, u32[]{:S(2)}) copy-start(pred[64]{0:T(512)(128)(4,1)} %get-tuple-element.19) | copy-start | bytes 196
  12.2 3.5 %copy-start.20 = (pred[64]{0:T(512)(128)(4,1)S(1)}, pred[64]{0:T(512)(128)(4,1)}, u32[]{:S(2)}) copy-start(pred[64]{0:T(512)(128)(4,1)} %get-tuple-element.20) | copy-start | bytes 196
  44.7 25.9 %copy-start.1 = (f32[4,16,64,256]{3,2,1,0:T(8,128)}, f32[4,16,64,256]{3,2,1,0:T(8,128)S(1)}, u32[]{:S(2)}) copy-start(f32[4,16,64,256]{3,2,1,0:T(8,128)S(1)} %fusion.6) | copy-start | bytes 12582916
  65.7 2.3 %copy-start.9 = (f32[4,12,128,128]{3,2,1,0:T(8,128)}, f32[4,12,128,128]{3,2,1,0:T(8,128)S(1)}, u32[]{:S(2)}) copy-start(f32[4,12,128,128]{3,2,1,0:T(8,128)S(1)} %fusion.24) | copy-start | bytes 9437188
  67.9 2.7 %copy-start.13 = (f32[4,8,128,128]{3,2,1,0:T(8,128)}, f32[4,8,128,128]{3,2,1,0:T(8,128)S(1)}, u32[]{:S(2)}) copy-start(f32[4,8,128,128]{3,2,1,0:T(8,128)S(1)} %fusion.107) | copy-start | bytes 6291460
  68.7 51.9 %collective-permute-start = (f32[4,128,128]{2,1,0:T(8,128)}, f32[4,128,128]{2,1,0:T(8,128)}, u32[]{:S(2)}, u32[]{:S(2)}) collective-permute-start(f32[4,128,128]{2,1,0:T(8,128)} %slice_bitcast_fusion.2), channel_id=1, source_target_pairs={{0,4},{4,8},{8,12},{12,16},{16,20},{20,24},{24,28},{28,32},{32,36}... | collective-permute-start | bytes 786440 | tf_op jit(solution)/shard_map/ppermute | solution.py:99
  88.8 2.0 copy-start.7
  90.8 4.0 %copy-start.4 = (f32[4,16,128,128]{3,2,0,1:T(8,128)}, f32[4,16,128,128]{3,2,0,1:T(8,128)S(1)}, u32[]{:S(2)}) copy-start(f32[4,16,128,128]{3,2,0,1:T(8,128)S(1)} %fusion) | copy-start | bytes 12582916
  90.8 4.0 %copy-start.10 = (f32[4,12,128,128]{3,2,1,0:T(8,128)S(1)}, f32[4,12,128,128]{3,2,1,0:T(8,128)}, u32[]{:S(2)}) copy-start(f32[4,12,128,128]{3,2,1,0:T(8,128)} %copy-done.9) | copy-start | bytes 9437188
  99.2 4.9 %copy-start.8 = (f32[4,8,128,128]{3,2,0,1:T(8,128)}, f32[4,8,128,128]{3,2,0,1:T(8,128)S(1)}, u32[]{:S(2)}) copy-start(f32[4,8,128,128]{3,2,0,1:T(8,128)S(1)} %slice_add_fusion.2) | copy-start | bytes 6291460
  100.0 27.0 %collective-permute-start.5 = (f32[4,128,128]{2,1,0:T(8,128)}, f32[4,128,128]{2,1,0:T(8,128)}, u32[]{:S(2)}, u32[]{:S(2)}) collective-permute-start(f32[4,128,128]{2,1,0:T(8,128)} %slice_bitcast_fusion), channel_id=1, source_target_pairs={{0,4},{4,8},{8,12},{12,16},{16,20},{20,24},{24,28},{28,32},{32,36}... | collective-permute-start | bytes 786440 | tf_op jit(solution)/shard_map/ppermute | solution.py:99
  108.4 3.4 %copy-start.2 = (f32[4,16,64,256]{3,2,1,0:T(8,128)S(1)}, f32[4,16,64,256]{3,2,1,0:T(8,128)}, u32[]{:S(2)}) copy-start(f32[4,16,64,256]{3,2,1,0:T(8,128)} %copy-done.1) | copy-start | bytes 12582916
  111.8 2.1 copy-start.5
  120.7 12.2 %copy-start.11 = (f32[4,8,128,128]{3,2,1,0:T(8,128)S(1)}, f32[4,8,128,128]{3,2,1,0:T(8,128)}, u32[]{:S(2)}) copy-start(f32[4,8,128,128]{3,2,1,0:T(8,128)} %get-tuple-element.7) | copy-start | bytes 6291460
  123.2 17.4 %collective-permute-start.1 = (f32[4,128,128]{2,1,0:T(8,128)}, f32[4,128,128]{2,1,0:T(8,128)}, u32[]{:S(2)}, u32[]{:S(2)}) collective-permute-start(f32[4,128,128]{2,1,0:T(8,128)} %convolution_select_fusion.8), channel_id=1, source_target_pairs={{0,8},{4,12},{8,16},{12,20},{16,24},{20,28},{24,32},{28,36},{32,40... | collective-permute-start | bytes 786440 | tf_op jit(solution)/shard_map/ppermute | solution.py:99
  129.3 16.7 %collective-permute-start.6 = (f32[4,128,128]{2,1,0:T(8,128)}, f32[4,128,128]{2,1,0:T(8,128)}, u32[]{:S(2)}, u32[]{:S(2)}) collective-permute-start(f32[4,128,128]{2,1,0:T(8,128)} %fusion.80), channel_id=1, source_target_pairs={{0,8},{4,12},{8,16},{12,20},{16,24},{20,28},{24,32},{28,36},{32,40... | collective-permute-start | bytes 786440 | tf_op jit(solution)/shard_map/ppermute | solution.py:99
  142.2 12.6 %collective-permute-start.2 = (f32[4,128,128]{2,1,0:T(8,128)S(1)}, f32[4,128,128]{2,1,0:T(8,128)S(1)}, u32[]{:S(2)}, u32[]{:S(2)}) collective-permute-start(f32[4,128,128]{2,1,0:T(8,128)S(1)} %convolution_select_fusion.6), channel_id=1, source_target_pairs={{0,16},{4,20},{8,24},{12,28},{16,32},{20,36},{24,40},{28,44},{32,4... | collective-permute-start | bytes 786440 | tf_op jit(solution)/shard_map/ppermute | solution.py:99
  147.5 13.1 %collective-permute-start.7 = (f32[4,128,128]{2,1,0:T(8,128)S(1)}, f32[4,128,128]{2,1,0:T(8,128)S(1)}, u32[]{:S(2)}, u32[]{:S(2)}) collective-permute-start(f32[4,128,128]{2,1,0:T(8,128)S(1)} %fusion.79), channel_id=1, source_target_pairs={{0,16},{4,20},{8,24},{12,28},{16,32},{20,36},{24,40},{28,44},{32,4... | collective-permute-start | bytes 786440 | tf_op jit(solution)/shard_map/ppermute | solution.py:99
  155.2 10.5 %collective-permute-start.3 = (f32[4,128,128]{2,1,0:T(8,128)S(1)}, f32[4,128,128]{2,1,0:T(8,128)S(1)}, u32[]{:S(2)}, u32[]{:S(2)}) collective-permute-start(f32[4,128,128]{2,1,0:T(8,128)S(1)} %convolution_select_fusion.4), channel_id=1, source_target_pairs={{0,32},{4,36},{8,40},{12,44},{16,48},{20,52},{24,56},{28,60},{32,6... | collective-permute-start | bytes 786440 | tf_op jit(solution)/shard_map/ppermute | solution.py:99
  161.0 9.8 %collective-permute-start.8 = (f32[4,128,128]{2,1,0:T(8,128)S(1)}, f32[4,128,128]{2,1,0:T(8,128)S(1)}, u32[]{:S(2)}, u32[]{:S(2)}) collective-permute-start(f32[4,128,128]{2,1,0:T(8,128)S(1)} %fusion.78), channel_id=1, source_target_pairs={{0,32},{4,36},{8,40},{12,44},{16,48},{20,52},{24,56},{28,60},{32,6... | collective-permute-start | bytes 786440 | tf_op jit(solution)/shard_map/ppermute | solution.py:99
  166.1 11.5 %collective-permute-start.4 = (f32[4,128,128]{2,1,0:T(8,128)S(1)}, f32[4,128,128]{2,1,0:T(8,128)S(1)}, u32[]{:S(2)}, u32[]{:S(2)}) collective-permute-start(f32[4,128,128]{2,1,0:T(8,128)S(1)} %convolution_select_fusion.2), channel_id=1, source_target_pairs={{0,64},{4,68},{8,72},{12,76},{16,80},{20,84},{24,88},{28,92},{32,9... | collective-permute-start | bytes 786440 | tf_op jit(solution)/shard_map/ppermute | solution.py:99
  171.2 10.3 %collective-permute-start.9 = (f32[4,128,128]{2,1,0:T(8,128)S(1)}, f32[4,128,128]{2,1,0:T(8,128)S(1)}, u32[]{:S(2)}, u32[]{:S(2)}) collective-permute-start(f32[4,128,128]{2,1,0:T(8,128)S(1)} %fusion.77), channel_id=1, source_target_pairs={{0,64},{4,68},{8,72},{12,76},{16,80},{20,84},{24,88},{28,92},{32,9... | collective-permute-start | bytes 786440 | tf_op jit(solution)/shard_map/ppermute | solution.py:99
  172.9 9.0 %copy-start.12 = (f32[4,16,32,128]{3,2,1,0:T(8,128)S(1)}, f32[4,16,32,128]{3,2,1,0:T(8,128)}, u32[]{:S(2)}) copy-start(f32[4,16,32,128]{3,2,1,0:T(8,128)} %fusion.2) | copy-start | bytes 3145732
  183.0 23.5 %collective-permute-start.12 = (bf16[512,512]{0,1:T(8,128)(2,1)S(1)}, bf16[512,512]{0,1:T(8,128)(2,1)S(1)}, u32[]{:S(2)}, u32[]{:S(2)}) collective-permute-start(bf16[512,512]{0,1:T(8,128)(2,1)S(1)} %bitcast.100), channel_id=1, source_target_pairs={{0,3},{1,0},{2,1},{3,2},{4,7},{5,4},{6,5},{7,6},{8,11},{9,8},{10,9... | collective-permute-start | bytes 1572872 | tf_op jit(solution)/shard_map/ppermute | solution.py:155
  186.0 23.8 %collective-permute-start.10 = (bf16[512,512]{0,1:T(8,128)(2,1)S(1)}, bf16[512,512]{0,1:T(8,128)(2,1)S(1)}, u32[]{:S(2)}, u32[]{:S(2)}) collective-permute-start(bf16[512,512]{0,1:T(8,128)(2,1)S(1)} %bitcast.101), channel_id=1, source_target_pairs={{0,1},{1,2},{2,3},{3,0},{4,5},{5,6},{6,7},{7,4},{8,9},{9,10},{10,1... | collective-permute-start | bytes 1572872 | tf_op jit(solution)/shard_map/ppermute | solution.py:155
  186.1 25.5 %collective-permute-start.11 = (bf16[512,512]{0,1:T(8,128)(2,1)S(1)}, bf16[512,512]{0,1:T(8,128)(2,1)S(1)}, u32[]{:S(2)}, u32[]{:S(2)}) collective-permute-start(bf16[512,512]{0,1:T(8,128)(2,1)S(1)} %bitcast.102), channel_id=1, source_target_pairs={{0,2},{1,3},{2,0},{3,1},{4,6},{5,7},{6,4},{7,5},{8,10},{9,11},{10,... | collective-permute-start | bytes 1572872 | tf_op jit(solution)/shard_map/ppermute | solution.py:155
  (4 other events, 7.0 us)
